TPU v7x, 256 devices: a whole 4x4x8 slice. The times are simulated.
256 devices in a mesh: seq: 16 (over x, y), grp: 16 (over z, core).
Axes of the slice: x: 4, y: 4, z: 8, core: 2. Of those that a mesh axis runs over, the one named last changes fastest.
Arguments:
- query_rows: bfloat16 [16, 2048, 4096], P('grp', 'seq'), may hold values from -6 to 6
- key_rows: bfloat16 [16, 2048, 1024], P('grp', 'seq'), may hold values from -6 to 6
- value_rows: bfloat16 [16, 2048, 1024], P('grp', 'seq'), may hold values from -27 to 27
- doc_of_block: int32 [16, 16], P('grp'), may hold values from 0 to 3, never falling along the last dimension, each value on 1 to 8 neighbouring positions
- expert_ids: int32 [16, 2048, 2], P('grp', 'seq'), may hold values from 0 to 7, as said below
- gate_weights: float32 [16, 2048, 2], P('grp', 'seq'), may hold values from 0.1 to 0.9
- norm_gain: float32 [4096], replicated, may hold values from 0.1 to 1.9
- w_in: bfloat16 [2, 7168, 4096], P(None, ('seq', 'grp')), may hold values from -0.09375 to 0.09375
- w_down: bfloat16 [7168, 4096], P(('seq', 'grp')), may hold values from -0.0625 to 0.0625
Outputs:
- layer_out: bfloat16 [16, 2048, 4096], P('grp', 'seq')
Inputs may be any that keep to these rules, and one draw needn't show every extreme that they name: `expert_ids`: each token names 2 different experts; in each aligned block of 128 tokens along a sequence (the tokens of one device) at most 40 tokens name expert 0, and in every draw some block has exactly 40 such tokens.
All inputs are finite; a program needn't handle non-finite values.
Results may differ from a plain program's by a relative error of at most 0.014.
Values may be sent and summed in bfloat16 or wider, within the bound.
No kernel may reach another device: no remote copies, remote signals or barrier semaphores. Data moves between devices by JAX's collectives and lax.ppermute only.
A program may use at most 128 MiB of HBM per device.

v0:
```python
import math

import jax
import jax.numpy as jnp
from jax import lax
from jax.sharding import PartitionSpec as P

QH = 32
KVH = 8
HD = 128
BLK = 128
CAP = 40


EPS = 1e-05
NEG = -1e30


def project_in(gathered, piece):
    return jnp.einsum("rd,khd->krh", gathered, piece, preferred_element_type=jnp.float32)


def activate(gate_up):
    return (jax.nn.silu(gate_up[0]) * gate_up[1]).astype(jnp.bfloat16)


def add_down(hidden, piece):
    return jnp.dot(hidden, piece, preferred_element_type=jnp.float32)


def attend(query_all, key_all, value_all, token_doc, per_dev, kv_local):
    seq_length = query_all.shape[1]
    tile_rows = min(512, seq_length)
    tile_count = seq_length // tile_rows
    per_kv = per_dev // kv_local
    inv_root = 1.0 / math.sqrt(HD)
    query_split = query_all[0].reshape(seq_length, kv_local, per_kv, HD)
    key_split = key_all[0].reshape(seq_length, kv_local, HD)
    value_split = value_all[0].reshape(seq_length, kv_local, HD)
    outputs = []
    for q_index in range(tile_count):
        query_tile = query_split[q_index * tile_rows : (q_index + 1) * tile_rows]
        doc_query = token_doc[q_index * tile_rows : (q_index + 1) * tile_rows]
        allowed_row = doc_query[:, None] == token_doc[None, :]
        scores = (
            jnp.einsum("qkgd,tkd->kgqt", query_tile, key_split, preferred_element_type=jnp.float32)
            * inv_root
        )
        scores = jnp.where(allowed_row, scores, NEG)
        highest = jnp.max(scores, axis=3, keepdims=True)
        weights = jnp.exp(scores - highest)
        denom = jnp.sum(weights, axis=3, keepdims=True)
        mixed = jnp.einsum(
            "kgqt,tkd->qkgd",
            weights.astype(jnp.bfloat16),
            value_split,
            preferred_element_type=jnp.float32,
        )
        mixed = mixed / jnp.transpose(denom, (2, 0, 1, 3))
        outputs.append(mixed.reshape(tile_rows, per_dev * HD).astype(jnp.bfloat16))
    return jnp.concatenate(outputs, axis=0)[None]


def shards(
    query_rows,
    key_rows,
    value_rows,
    doc_of_block,
    expert_ids,
    gate_weights,
    norm_gain,
    w_in,
    w_down,
):
    seq_count = lax.axis_size("seq")
    tok_count = query_rows.shape[1]
    per_dev = QH // seq_count
    repeat_count = max(1, 4 // per_dev)
    kv_local = KVH * repeat_count // seq_count
    key_send = jnp.repeat(key_rows.reshape(1, tok_count, KVH, HD), repeat_count, axis=2).reshape(
        1, tok_count, KVH * repeat_count * HD
    )
    value_send = jnp.repeat(
        value_rows.reshape(1, tok_count, KVH, HD), repeat_count, axis=2
    ).reshape(1, tok_count, KVH * repeat_count * HD)
    query_all, key_all, value_all = (
        lax.all_to_all(query_rows, "seq", split_axis=2, concat_axis=1, tiled=True),
        lax.all_to_all(key_send, "seq", split_axis=2, concat_axis=1, tiled=True),
        lax.all_to_all(value_send, "seq", split_axis=2, concat_axis=1, tiled=True),
    )
    token_doc = jnp.repeat(doc_of_block[0], BLK)
    attended = attend(query_all, key_all, value_all, token_doc, per_dev, kv_local)
    attn_tokens = lax.all_to_all(attended, "seq", split_axis=1, concat_axis=2, tiled=True)
    attn_float = attn_tokens[0].astype(jnp.float32)
    spread = jnp.mean(attn_float * attn_float, axis=-1, keepdims=True)
    normed = (attn_float * lax.rsqrt(spread + EPS) * norm_gain).astype(jnp.bfloat16)
    chosen = expert_ids[0] == 0
    routed = jnp.any(chosen, axis=-1)
    gate_share = jnp.sum(jnp.where(chosen, gate_weights[0], 0.0), axis=-1)
    slot_index = jnp.cumsum(routed.astype(jnp.int32)) - 1
    onehot = (slot_index[None, :] == jnp.arange(CAP, dtype=jnp.int32)[:, None]) & routed[None, :]
    dispatched = jnp.dot(
        onehot.astype(jnp.bfloat16), normed, preferred_element_type=jnp.float32
    ).astype(jnp.bfloat16)
    gathered = lax.all_gather(dispatched, "grp", axis=0, tiled=True)
    gate_up = project_in(gathered, lax.all_gather(w_in, "seq", axis=1, tiled=True))
    hidden = activate(gate_up)
    terms = add_down(hidden, lax.all_gather(w_down, "seq", axis=0, tiled=True))
    returned = lax.psum_scatter(
        terms.astype(jnp.bfloat16), "grp", scatter_dimension=0, tiled=True
    ).astype(jnp.float32)
    picked_rows = jnp.take(returned, jnp.clip(slot_index, 0, CAP - 1), axis=0)
    expert_out = jnp.where(routed[:, None], picked_rows, 0.0)
    layer_out = attn_float + gate_share[:, None] * expert_out
    return layer_out.astype(jnp.bfloat16)[None]


def solution(mesh):
    return jax.shard_map(
        shards,
        mesh=mesh,
        in_specs=(
            P("grp", "seq", None),
            P("grp", "seq", None),
            P("grp", "seq", None),
            P("grp", None),
            P("grp", "seq", None),
            P("grp", "seq", None),
            P(),
            P(None, ("seq", "grp"), None),
            P(("seq", "grp"), None),
        ),
        out_specs=P("grp", "seq", None),
        check_vma=False,
    )
```

profile of v0, /device:TPU:2, one launch (start us, length us, event | category | flops | bytes accessed | tf_op | source)
XLA Modules:
  0.0 441.8 jit_solution(3743156761703894871)
XLA Ops:
  6.5 1.2 copy.112
  7.9 8.1 %copy.145 = bf16[1,128,2048]{1,0,2:T(2,128)(2,1)S(1)} copy(bf16[1,128,2048]{1,2,0:T(8,128)(2,1)S(1)} %bitcast.306) | data formatting | bytes 1048576 | tf_op jit(solution)/shard_map/broadcast_in_dim | solution.py:80
  16.5 11.5 %reduce.20 = bf16[2048,128]{1,0:T(8,128)(2,1)S(1)} reduce(bf16[2048,1,128]{2,1,0:T(2,128)(2,1)S(1)} %bitcast.304, bf16[]{:T(256)} %broadcast.226), dimensions={1}, to_apply=%bitcast.292.reduce_sub_computation | reduce | bytes 1048578
  29.0 7.5 %all-to-all-start = ((bf16[16,2,8192]{2,1,0:T(2,128)(2,1)}), bf16[16,2,8192]{2,1,0:T(2,128)(2,1)S(1)}, u32[]{:S(2)}, u32[]{:S(2)}) async-start(bf16[16,2,8192]{2,1,0:T(2,128)(2,1)} %reshape.333), calls=%async_computation | async-start | bytes 1048576 | tf_op jit(solution)/shard_map/all_to_all | solution.py:88
  36.5 10.8 %all-gather.9.cloned.1.call-start = ((), (), s32[]{:S(2)}) async-start(), calls=%async_computation.8 | async-start | bytes 4456448 | tf_op jit(solution)/shard_map/all_gather | solution.py:108
  47.3 1.1 copy.113
  48.5 8.1 %copy.144 = bf16[1,128,2048]{1,0,2:T(2,128)(2,1)S(1)} copy(bf16[1,128,2048]{1,2,0:T(8,128)(2,1)S(1)} %bitcast.307) | data formatting | bytes 1048576 | tf_op jit(solution)/shard_map/broadcast_in_dim | solution.py:83
  56.6 11.5 %reduce.19 = bf16[2048,128]{1,0:T(8,128)(2,1)S(1)} reduce(bf16[2048,1,128]{2,1,0:T(2,128)(2,1)S(1)} %bitcast.305, bf16[]{:T(256)} %broadcast.226), dimensions={1}, to_apply=%bitcast.291.reduce_sub_computation | reduce | bytes 1048578
  69.1 7.2 %all-to-all-start.2 = ((bf16[16,2,8192]{2,1,0:T(2,128)(2,1)}), bf16[16,2,8192]{2,1,0:T(2,128)(2,1)}, u32[]{:S(2)}, u32[]{:S(2)}) async-start(bf16[16,2,8192]{2,1,0:T(2,128)(2,1)} %reshape.331), calls=%async_computation.2 | async-start | bytes 1048576 | tf_op jit(solution)/shard_map/all_to_all | solution.py:89
  76.4 2.8 copy.84
  79.2 22.4 %reduce.21 = bf16[4096,128]{1,0:T(8,128)(2,1)S(1)} reduce(bf16[4096,1,128]{2,1,0:T(2,128)(2,1)S(1)} %bitcast.299, bf16[]{:T(256)} %broadcast.226), dimensions={1}, to_apply=%bitcast.272.reduce_sub_computation | reduce | bytes 2097154
  101.6 1.1 reshape.335
  102.9 7.7 %all-to-all-start.1 = ((bf16[16,2,16384]{2,1,0:T(2,128)(2,1)}), bf16[16,2,16384]{2,1,0:T(2,128)(2,1)S(1)}, u32[]{:S(2)}, u32[]{:S(2)}) async-start(bf16[16,2,16384]{2,1,0:T(2,128)(2,1)} %reshape.335), calls=%async_computation.1 | async-start | bytes 2097152 | tf_op jit(solution)/shard_map/all_to_all | solution.py:87
  110.7 3.8 broadcast_compare_fusion.3
  114.5 2.2 reshape.334
  117.8 2.2 reshape.332
  121.5 3.1 all-to-all-done.1
  126.1 3.3 fusion.10
  129.4 2.0 fusion
  131.5 2.6 fusion.59
  134.4 2.9 fusion.11
  137.4 2.2 fusion.2
  139.6 2.6 fusion.65
  142.6 2.9 fusion.12
  145.5 2.0 fusion.4
  147.6 3.3 fusion.71
  152.2 2.2 fusion.13
  154.4 2.2 fusion.6
  156.7 2.6 fusion.77
  159.5 11.7 %copy.143 = bf16[1,2048,256]{2,0,1:T(2,128)(2,1)S(1)} copy(bf16[1,2048,256]{2,1,0:T(8,128)(2,1)S(1)} %maximum_bitcast_fusion) | data formatting | bytes 2097152 | tf_op jit(solution)/shard_map/broadcast_in_dim | solution.py:61
  171.3 10.6 %reduce.22 = bf16[2048,256]{1,0:T(8,128)(2,1)S(1)} reduce(bf16[2048,1,256]{2,1,0:T(2,128)(2,1)S(1)} %bitcast.297, bf16[]{:T(256)} %broadcast.226), dimensions={1}, to_apply=%bitcast.290.reduce_sub_computation | reduce | bytes 2097154
  181.9 1.1 reshape.337
  183.0 5.6 %all-to-all-start.3 = ((bf16[16,2,16384]{2,1,0:T(2,128)(2,1)}), bf16[16,2,16384]{2,1,0:T(2,128)(2,1)S(1)}, u32[]{:S(2)}, u32[]{:S(2)}) async-start(bf16[16,2,16384]{2,1,0:T(2,128)(2,1)} %reshape.337), calls=%async_computation.3 | async-start | bytes 2097152 | tf_op jit(solution)/shard_map/all_to_all | solution.py:93
  189.1 13.6 %all-to-all-done.3 = bf16[16,2,16384]{2,1,0:T(2,128)(2,1)S(1)} async-done(((bf16[16,2,16384]{2,1,0:T(2,128)(2,1)}), bf16[16,2,16384]{2,1,0:T(2,128)(2,1)S(1)}, u32[]{:S(2)}, u32[]{:S(2)}) %all-to-all-start.3) | async-done | bytes 1048608 | tf_op jit(solution)/shard_map/all_to_all | solution.py:93
  203.7 1.2 copy.105
  205.0 1.6 copy.117
  206.6 15.4 %multiply_reduce_fusion = f32[2048]{0:T(1024)S(1)} fusion(bf16[2048,1,256]{2,1,0:T(2,128)(2,1)S(1)} %reshape.338), kind=kLoop, calls=%fused_computation.44 | loop fusion | flops 1570816 | bytes 1056768 | tf_op jit(solution)/shard_map/reduce_sum | solution.py:95
  222.1 1.1 convolution_convert_fusion.1
  224.0 5.1 %reshape.324 = bf16[448,4096]{1,0:T(8,128)(2,1)} reshape(bf16[16,28,4096]{2,1,0:T(8,128)(2,1)} %all-gather.9.cloned.1.call-done) | data formatting | bytes 7340032
  229.1 38.4 %all-gather.5.cloned.1.call-done = bf16[640,4096]{1,0:T(8,128)(2,1)} async-done(((bf16[40,4096]{1,0:T(8,128)(2,1)}), bf16[640,4096]{1,0:T(8,128)(2,1)}) %all-gather.5.cloned.1.call-update) | async-done | bytes 5242896 | tf_op jit(solution)/shard_map/all_gather | solution.py:105
  267.5 72.1 %all-gather.7.cloned.1.call-done = bf16[2,448,4096]{2,0,1:T(2,128)(2,1)} async-done(((bf16[2,28,4096]{2,0,1:T(2,128)(2,1)}), bf16[2,448,4096]{2,0,1:T(2,128)(2,1)}) %all-gather.7.cloned.1.call-update) | async-done | bytes 7340048 | tf_op jit(solution)/shard_map/all_gather | solution.py:106
  339.6 18.5 %fusion.35 = f32[2,640,448]{1,2,0:T(8,128)S(1)} fusion(bf16[2,448,4096]{2,0,1:T(2,128)(2,1)} %all-gather.7.cloned.1.call-done, bf16[640,4096]{1,0:T(8,128)(2,1)} %all-gather.5.cloned.1.call-done), kind=kOutput, calls=%fused_computation.49 | convolution fusion | flops 4697620480 | bytes 14876672 | tf_op jit(solution)/shard_map/rd,khd->krh/dot_general | solution.py:20
  358.2 4.8 %convolution_convert_fusion = bf16[640,4096]{1,0:T(8,128)(2,1)} fusion(bf16[448,4096]{1,0:T(8,128)(2,1)S(1)} %copy-done.4, f32[2,640,448]{1,2,0:T(8,128)S(1)} %fusion.35), kind=kOutput, calls=%fused_computation.23 | convolution fusion | flops 2353152000 | bytes 11206656 | tf_op jit(solution)/shard_map/dot_general | solution.py:28
  363.0 2.6 copy.142
  365.6 1.7 reshape.310
  367.4 60.8 %reduce-scatter.2.cloned.1.call-done = bf16[40,4096]{1,0:T(8,128)(2,1)} async-done(((bf16[640,4096]{1,0:T(8,128)(2,1)}), bf16[40,4096]{1,0:T(8,128)(2,1)}) %reduce-scatter.2.cloned.1.call-update) | async-done | bytes 327696 | tf_op jit(solution)/shard_map/reduce_scatter | solution.py:109
  429.2 2.6 gather_fusion
  431.7 3.1 fusion.34
  (84 shorter events, 12.5 us)
Async XLA Ops:
  6.5 69.8 %copy-start.13 = (s32[1,16]{1,0:T(1,128)S(1)}, s32[1,16]{1,0:T(1,128)}, u32[]{:S(2)}) copy-start(s32[1,16]{1,0:T(1,128)} %param.12) | copy-start | bytes 196
  6.5 69.9 %copy-start.6 = (bf16[1,128,4096]{2,1,0:T(8,128)(2,1)S(1)}, bf16[1,128,4096]{2,1,0:T(8,128)(2,1)}, u32[]{:S(2)}) copy-start(bf16[1,128,4096]{2,1,0:T(8,128)(2,1)} %param.9) | copy-start | bytes 3145732
  29.0 40.1 %all-to-all-start = ((bf16[16,2,8192]{2,1,0:T(2,128)(2,1)}), bf16[16,2,8192]{2,1,0:T(2,128)(2,1)S(1)}, u32[]{:S(2)}, u32[]{:S(2)}) async-start(bf16[16,2,8192]{2,1,0:T(2,128)(2,1)} %reshape.333), calls=%async_computation | async-start | bytes 1048576 | tf_op jit(solution)/shard_map/all_to_all | solution.py:88
  36.5 187.5 %all-gather.9.cloned.1.call-start = ((), (), s32[]{:S(2)}) async-start(), calls=%async_computation.8 | async-start | bytes 4456448 | tf_op jit(solution)/shard_map/all_gather | solution.py:108
  69.1 7.2 %copy-start.5 = (bf16[16,2,8192]{2,1,0:T(2,128)(2,1)}, bf16[16,2,8192]{2,1,0:T(2,128)(2,1)S(1)}, u32[]{:S(2)}) copy-start(bf16[16,2,8192]{2,1,0:T(2,128)(2,1)S(1)} %all-to-all-done) | copy-start | bytes 1572868
  69.1 33.8 %all-to-all-start.2 = ((bf16[16,2,8192]{2,1,0:T(2,128)(2,1)}), bf16[16,2,8192]{2,1,0:T(2,128)(2,1)}, u32[]{:S(2)}, u32[]{:S(2)}) async-start(bf16[16,2,8192]{2,1,0:T(2,128)(2,1)} %reshape.331), calls=%async_computation.2 | async-start | bytes 1048576 | tf_op jit(solution)/shard_map/all_to_all | solution.py:89
  102.9 21.7 %all-to-all-start.1 = ((bf16[16,2,16384]{2,1,0:T(2,128)(2,1)}), bf16[16,2,16384]{2,1,0:T(2,128)(2,1)S(1)}, u32[]{:S(2)}, u32[]{:S(2)}) async-start(bf16[16,2,16384]{2,1,0:T(2,128)(2,1)} %reshape.335), calls=%async_computation.1 | async-start | bytes 2097152 | tf_op jit(solution)/shard_map/all_to_all | solution.py:87
  125.8 3.6 copy-start.3
  126.1 5.3 %copy-start.8 = (bf16[2048,128,1]{0,1,2:T(8,128)(2,1)S(1)}, bf16[2048,128,1]{0,1,2:T(8,128)(2,1)}, u32[]{:S(2)}) copy-start(bf16[2048,128,1]{0,1,2:T(8,128)(2,1)} %reshape.326) | copy-start | bytes 1572868
  131.4 3.0 copy-start.2
  134.4 5.1 %copy-start.9 = (bf16[2048,128,1]{0,1,2:T(8,128)(2,1)S(1)}, bf16[2048,128,1]{0,1,2:T(8,128)(2,1)}, u32[]{:S(2)}) copy-start(bf16[2048,128,1]{0,1,2:T(8,128)(2,1)} %reshape.326) | copy-start | bytes 1572868
  139.6 3.0 copy-start.1
  142.6 5.0 %copy-start.10 = (bf16[2048,128,1]{0,1,2:T(8,128)(2,1)S(1)}, bf16[2048,128,1]{0,1,2:T(8,128)(2,1)}, u32[]{:S(2)}) copy-start(bf16[2048,128,1]{0,1,2:T(8,128)(2,1)} %reshape.326) | copy-start | bytes 1572868
  147.5 4.6 %copy-start = (pred[512,2048]{0,1:T(8,128)(4,1)S(1)}, pred[512,2048]{0,1:T(8,128)(4,1)}, u32[]{:S(2)}) copy-start(pred[512,2048]{0,1:T(8,128)(4,1)} %get-tuple-element.14) | copy-start | bytes 3145732
  147.6 4.6 %copy-start.7 = (bf16[1,16,128,128]{3,2,1,0:T(8,128)(2,1)S(1)}, bf16[1,16,128,128]{3,2,1,0:T(8,128)(2,1)}, u32[]{:S(2)}) copy-start(bf16[1,16,128,128]{3,2,1,0:T(8,128)(2,1)} %copy.83) | copy-start | bytes 1572868
  152.2 4.5 %copy-start.11 = (bf16[2048,128,1]{0,1,2:T(8,128)(2,1)S(1)}, bf16[2048,128,1]{0,1,2:T(8,128)(2,1)}, u32[]{:S(2)}) copy-start(bf16[2048,128,1]{0,1,2:T(8,128)(2,1)} %reshape.326) | copy-start | bytes 1572868
  159.3 29.3 %copy-start.14 = (s32[1,128,2]{1,2,0:T(2,128)S(1)}, s32[1,128,2]{1,2,0:T(2,128)}, u32[]{:S(2)}) copy-start(s32[1,128,2]{1,2,0:T(2,128)} %param.13) | copy-start | bytes 3076
  183.0 39.1 %copy-start.12 = (f32[4096]{0:T(1024)S(1)}, f32[4096]{0:T(1024)}, u32[]{:S(2)}) copy-start(f32[4096]{0:T(1024)} %param.15) | copy-start | bytes 49156
  183.0 19.7 %all-to-all-start.3 = ((bf16[16,2,16384]{2,1,0:T(2,128)(2,1)}), bf16[16,2,16384]{2,1,0:T(2,128)(2,1)S(1)}, u32[]{:S(2)}, u32[]{:S(2)}) async-start(bf16[16,2,16384]{2,1,0:T(2,128)(2,1)} %reshape.337), calls=%async_computation.3 | async-start | bytes 2097152 | tf_op jit(solution)/shard_map/all_to_all | solution.py:93
  188.6 78.9 %all-gather.5.cloned.1.call-start = ((), (), s32[]{:S(2)}) async-start(), calls=%async_computation.5 | async-start | bytes 5570560 | tf_op jit(solution)/shard_map/all_gather | solution.py:105
  223.2 116.4 %all-gather.7.cloned.1.call-start = ((), (), s32[]{:S(2)}) async-start(), calls=%async_computation.6 | async-start | bytes 7798784 | tf_op jit(solution)/shard_map/all_gather | solution.py:106
  223.9 204.2 %reduce-scatter.2.cloned.1.call-start = ((), (), s32[]{:S(2)}) async-start(), calls=%async_computation.7 | async-start | bytes 5570560 | tf_op jit(solution)/shard_map/reduce_scatter | solution.py:109
  339.6 18.6 %copy-start.4 = (bf16[448,4096]{1,0:T(8,128)(2,1)S(1)}, bf16[448,4096]{1,0:T(8,128)(2,1)}, u32[]{:S(2)}) copy-start(bf16[448,4096]{1,0:T(8,128)(2,1)} %reshape.324) | copy-start | bytes 11010052
  358.2 4.8 %copy-start.15 = (f32[1,128,2]{1,2,0:T(2,128)S(1)}, f32[1,128,2]{1,2,0:T(2,128)}, u32[]{:S(2)}) copy-start(f32[1,128,2]{1,2,0:T(2,128)} %param.14) | copy-start | bytes 3076
Sparse Core Ops, SparseCore 0:
  47.4 59.1 all-gather.8
  223.3 44.1 all-gather.4
  270.0 69.6 all-gather.6
  363.1 64.9 reduce-scatter.1
where the time goes:
time: 450 us; the launch traced here: 442 us
  waiting for transfers between devices  189 us (42%)
  other arithmetic  88.2 us (20%)
  local copies, waits for them, and re-layouts  64.8 us (14%)
  matrix products  46.9 us (10%)
  starting transfers between devices  38.9 us (9%)
  between operations  14.1 us (3%)
    all_gather x1, waiting for transfers between devices, shards(): lax.all_gather(w_in, 'seq', axis=1, tiled=True)  72.1 us
    reduce_scatter x1, waiting for transfers between devices, shards(): lax.psum_scatter(terms.astype(jnp.bfloat16), 'grp', scatter_dimension=0,...  60.8 us
    unnamed x4, other arithmetic  56 us
    all_gather x1, waiting for transfers between devices, shards(): gathered = lax.all_gather(dispatched, 'grp', axis=0, tiled=True)  38.4 us
    unnamed x47, local copies, waits for them, and re-layouts  21 us
    dot_general x1, matrix products, project_in(): jnp.einsum('rd,khd->krh', gathered, piece, preferred_element_type=jnp.flo...  18.5 us
    reduce_sum x2, other arithmetic, shards(): spread = jnp.mean(attn_float * attn_float, axis=-1, keepdims=True)  15.4 us
    all_to_all x1, waiting for transfers between devices, shards(): lax.all_to_all(attended, 'seq', split_axis=1, concat_axis=2, tiled=True)  13.6 us
  transfers between devices with their start and end apart: 8, of which 5 were waited for; matrix products, arithmetic and copies ran while one was open for 33% of the time, Pallas kernels for 0%

commit v1 on v0

v1 whole, which is shorter than its diff:
```python
import math

import jax
import jax.numpy as jnp
from jax import lax
from jax.sharding import PartitionSpec as P


QH = 32
KVH = 8
HD = 128
BLK = 128
CAP = 40


EPS = 1e-05
NEG = -1e30


def attend(query_all, key_all, value_all, token_doc, per_dev):
    seq_length = query_all.shape[0]
    tile_rows = min(512, seq_length)
    tile_count = seq_length // tile_rows
    inv_root = 1.0 / math.sqrt(HD)
    query_split = query_all.reshape(seq_length, per_dev, HD)
    outputs = []
    for q_index in range(tile_count):
        query_tile = query_split[q_index * tile_rows : (q_index + 1) * tile_rows]
        doc_query = token_doc[q_index * tile_rows : (q_index + 1) * tile_rows]
        allowed_row = doc_query[:, None] == token_doc[None, :]
        scores = (
            jnp.einsum("qgd,td->gqt", query_tile, key_all, preferred_element_type=jnp.float32)
            * inv_root
        )
        scores = jnp.where(allowed_row, scores, NEG)
        highest = jnp.max(scores, axis=2, keepdims=True)
        weights = jnp.exp(scores - highest)
        denom = jnp.sum(weights, axis=2, keepdims=True)
        mixed = jnp.einsum(
            "gqt,td->qgd",
            weights.astype(jnp.bfloat16),
            value_all,
            preferred_element_type=jnp.float32,
        )
        mixed = mixed / jnp.transpose(denom, (1, 0, 2))
        outputs.append(mixed.reshape(tile_rows, per_dev * HD).astype(jnp.bfloat16))
    return jnp.concatenate(outputs, axis=0)


def shards_body(
    query_rows,
    key_rows,
    value_rows,
    doc_of_block,
    expert_ids,
    gate_weights,
    norm_gain,
    w_in,
    w_down,
):
    seq_count = lax.axis_size("seq")
    tok_count = query_rows.shape[1]
    per_dev = QH // seq_count
    feat = per_dev * HD
    kv_of_dest = (jnp.arange(seq_count) * per_dev) // (QH // KVH)

    weights_local = jnp.concatenate([w_in, w_down[None]], axis=0)[None]
    weights_all = lax.all_gather(weights_local, "seq", axis=0, tiled=True)

    query_send = jnp.transpose(query_rows[0].reshape(tok_count, seq_count, feat), (1, 0, 2))
    key_send = jnp.transpose(key_rows[0].reshape(tok_count, KVH, HD)[:, kv_of_dest, :], (1, 0, 2))
    value_send = jnp.transpose(
        value_rows[0].reshape(tok_count, KVH, HD)[:, kv_of_dest, :], (1, 0, 2)
    )
    packed = jnp.concatenate([query_send, key_send, value_send], axis=2)
    packed_all = lax.all_to_all(packed, "seq", 0, 0, tiled=False)
    seq_length = seq_count * tok_count
    query_all = packed_all[:, :, :feat].reshape(seq_length, feat)
    key_all = packed_all[:, :, feat : feat + HD].reshape(seq_length, HD)
    value_all = packed_all[:, :, feat + HD :].reshape(seq_length, HD)

    token_doc = jnp.repeat(doc_of_block[0], BLK)
    attended = attend(query_all, key_all, value_all, token_doc, per_dev)
    attn_back = lax.all_to_all(
        attended.reshape(seq_count, tok_count, feat), "seq", 0, 0, tiled=False
    )
    attn_tokens = jnp.transpose(attn_back, (1, 0, 2)).reshape(tok_count, seq_count * feat)
    attn_float = attn_tokens.astype(jnp.float32)
    spread = jnp.mean(attn_float * attn_float, axis=-1, keepdims=True)
    normed = (attn_float * lax.rsqrt(spread + EPS) * norm_gain).astype(jnp.bfloat16)
    chosen = expert_ids[0] == 0
    routed = jnp.any(chosen, axis=-1)
    gate_share = jnp.sum(jnp.where(chosen, gate_weights[0], 0.0), axis=-1)
    slot_index = jnp.cumsum(routed.astype(jnp.int32)) - 1
    onehot = (slot_index[None, :] == jnp.arange(CAP, dtype=jnp.int32)[:, None]) & routed[None, :]
    dispatched = jnp.dot(
        onehot.astype(jnp.bfloat16), normed, preferred_element_type=jnp.float32
    ).astype(jnp.bfloat16)
    gathered = lax.all_gather(dispatched, "grp", axis=0, tiled=True)
    gate_up = jnp.einsum(
        "rd,jkud->krju", gathered, weights_all[:, :2], preferred_element_type=jnp.float32
    )
    hidden = (jax.nn.silu(gate_up[0]) * gate_up[1]).astype(jnp.bfloat16)
    terms = jnp.einsum(
        "rju,jud->rd", hidden, weights_all[:, 2], preferred_element_type=jnp.float32
    )
    returned = lax.psum_scatter(
        terms.astype(jnp.bfloat16), "grp", scatter_dimension=0, tiled=True
    ).astype(jnp.float32)
    picked_rows = jnp.take(returned, jnp.clip(slot_index, 0, CAP - 1), axis=0)
    expert_out = jnp.where(routed[:, None], picked_rows, 0.0)
    layer_out = attn_float + gate_share[:, None] * expert_out
    return layer_out.astype(jnp.bfloat16)[None]


def solution(mesh):
    return jax.shard_map(
        shards_body,
        mesh=mesh,
        in_specs=(
            P("grp", "seq", None),
            P("grp", "seq", None),
            P("grp", "seq", None),
            P("grp", None),
            P("grp", "seq", None),
            P("grp", "seq", None),
            P(),
            P(None, ("seq", "grp"), None),
            P(("seq", "grp"), None),
        ),
        out_specs=P("grp", "seq", None),
        check_vma=False,
    )
```

time: 450 us -> 348 us (0.77); the launches traced: 442 us -> 347 us
  other arithmetic: 88.2 us -> 22.1 us
  waiting for transfers between devices: 189 us -> 236 us
  local copies, waits for them, and re-layouts: 64.8 us -> 18.4 us
  starting transfers between devices: 38.9 us -> 14.4 us
    unnamed x4 -> x0, other arithmetic: 56 us -> none
    all_gather x3 -> x2, waiting for transfers between devices: 111 us -> 139 us  [the longest x1 95.8 us: shards_body(): weights_all = lax.all_gather(weights_local, 'seq', axis=0, tiled=True)]
    broadcast_in_dim x5 -> x0, local copies, waits for them, and re-layouts: 28.2 us -> none  [the longest x1 11.7 us: attend(): return jnp.concatenate(outputs, axis=0)[None]]
    all_to_all x4 -> x2, waiting for transfers between devices: 16.7 us -> 35.7 us  [the longest x1 23.2 us: shards_body(): packed_all = lax.all_to_all(packed, 'seq', 0, 0, tiled=False)]
    unnamed x47 -> x40, local copies, waits for them, and re-layouts: 21 us -> 4.07 us
    reduce_sum x7 -> x6, other arithmetic: 23.9 us -> 9 us  [the longest x4 8.42 us: attend(): denom = jnp.sum(weights, axis=2, keepdims=True)]
    all_to_all x4 -> x2, starting transfers between devices: 28 us -> 14.3 us  [the longest x1 7.48 us: shards_body(): packed_all = lax.all_to_all(packed, 'seq', 0, 0, tiled=False)]
    all_gather x3 -> x2, starting transfers between devices: 10.9 us -> 0.08 us  [the longest x1 0.04 us: shards_body(): weights_all = lax.all_gather(weights_local, 'seq', axis=0, tiled=True)]
  transfers between devices with their start and end apart: 8 -> 5, of which waited for: 5 -> 5; matrix products, arithmetic and copies ran while one was open for 33% -> 3% of each run, Pallas kernels for 0% -> 0%
where the time goes in v1:
time: 348 us; the launch traced here: 347 us
  waiting for transfers between devices  236 us (68%)
  matrix products  42.8 us (12%)
  other arithmetic  22.1 us (6%)
  local copies, waits for them, and re-layouts  18.4 us (5%)
  starting transfers between devices  14.4 us (4%)
  between operations  13.5 us (4%)
    all_gather x1, waiting for transfers between devices, shards_body(): weights_all = lax.all_gather(weights_local, 'seq', axis=0, tiled=True)  95.8 us
    reduce_scatter x1, waiting for transfers between devices, shards_body(): lax.psum_scatter(terms.astype(jnp.bfloat16), 'grp', scatter_dimension=0,...  61.6 us
    all_gather x1, waiting for transfers between devices, shards_body(): gathered = lax.all_gather(dispatched, 'grp', axis=0, tiled=True)  43.1 us
    all_to_all x1, waiting for transfers between devices, shards_body(): packed_all = lax.all_to_all(packed, 'seq', 0, 0, tiled=False)  23.2 us
    dot_general x4, matrix products, attend(): jnp.einsum('gqt,td->qgd', weights.astype(jnp.bfloat16), value_all, prefer...  12.6 us
    all_to_all x1, waiting for transfers between devices, shards_body(): lax.all_to_all(attended.reshape(seq_count, tok_count, feat), 'seq', 0, 0,...  12.4 us
    dot_general x4, matrix products, attend(): jnp.einsum('qgd,td->gqt', query_tile, key_all, preferred_element_type=jnp...  10.8 us
    dot_general x1, matrix products, shards_body(): jnp.einsum('rd,jkud->krju', gathered, weights_all[:, :2], preferred_eleme...  10.7 us
  transfers between devices with their start and end apart: 5, of which 5 were waited for; matrix products, arithmetic and copies ran while one was open for 3% of the time, Pallas kernels for 0%

profile of v1, /device:TPU:2, one launch (start us, length us, event | category | flops | bytes accessed | tf_op | source)
XLA Modules:
  0.0 347.4 jit_solution(3798032094915179123)
XLA Ops:
  6.6 1.1 copy.71
  7.7 0.2 copy.72
  7.9 1.1 copy.73
  9.0 0.2 copy.74
  9.2 0.7 gather_fusion
  9.9 0.6 gather_fusion.1
  10.5 1.5 copy.96
  12.0 0.3 copy.114
  12.3 1.6 pad_maximum_fusion
  14.0 7.5 %all-to-all-start = ((bf16[16,128,512]{2,1,0:T(8,128)(2,1)}), bf16[16,128,512]{2,1,0:T(8,128)(2,1)S(1)}, u32[]{:S(2)}, u32[]{:S(2)}) async-start(bf16[16,128,512]{2,1,0:T(8,128)(2,1)} %pad_maximum_fusion), calls=%async_computation | async-start | bytes 4194304 | tf_op jit(solution)/shard_map/all_to_all | solution.py:76
  21.7 3.7 %broadcast_compare_fusion.3 = (pred[512,2048]{0,1:T(8,128)(4,1)}, pred[512,2048]{0,1:T(8,128)(4,1)}, pred[512,2048]{0,1:T(8,128)(4,1)}, pred[512,2048]{0,1:T(8,128)(4,1)S(1)}) fusion(s32[512]{0:T(512)S(1)} %get-tuple-element.32, s32[2048]{0:T(1024)S(1)} %broadcast_bitcast_fusion, s32[512]{0:T(512)S(1)} %get-tuple-element.31, s32[512]{0:T(512)S(1)} %get-tuple-element.30, ...), kind=kLoop, calls=%fused_computation.49 | loop fusion | flops 4194304 | bytes 4210688 | tf_op jit(solution)/shard_map/eq | solution.py:30
  25.4 23.2 %all-to-all-done = bf16[16,128,512]{2,1,0:T(8,128)(2,1)S(1)} async-done(((bf16[16,128,512]{2,1,0:T(8,128)(2,1)}), bf16[16,128,512]{2,1,0:T(8,128)(2,1)S(1)}, u32[]{:S(2)}, u32[]{:S(2)}) %all-to-all-start) | async-done | bytes 2097184 | tf_op jit(solution)/shard_map/all_to_all | solution.py:76
  48.6 0.9 fusion.98
  49.5 1.7 slice.84
  51.3 1.7 slice.88
  53.0 0.3 fusion.99
  53.3 3.5 %fusion.8 = (f32[2,512]{1,0:T(2,128)S(1)}, f32[2048,512,2]{1,0,2:T(8,128)S(1)}) fusion(pred[512,2048]{0,1:T(8,128)(4,1)} %get-tuple-element.13, bf16[2048,128,1]{1,0,2:T(8,128)(2,1)S(1)} %bitcast.209, bf16[512,2,128]{2,1,0:T(2,128)(2,1)} %slice.84), kind=kOutput, calls=%fused_computation.20 | convolution fusion | flops 543161344 | bytes 10227712 | tf_op jit(solution)/shard_map/qgd,td->gqt/dot_general | solution.py:32
  56.8 2.0 fusion
  58.9 3.3 fusion.69
  62.2 2.2 fusion.9
  64.4 2.2 fusion.2
  66.7 3.3 fusion.63
  70.0 0.8 slice.92
  70.8 2.8 fusion.10
  73.6 2.0 fusion.4
  75.6 3.3 fusion.57
  79.0 2.2 fusion.11
  81.2 2.2 fusion.6
  83.5 2.6 fusion.51
  86.3 1.3 copy.84
  87.6 6.8 %all-to-all-start.1 = ((bf16[16,128,256]{2,1,0:T(8,128)(2,1)}), bf16[16,128,256]{2,1,0:T(8,128)(2,1)S(1)}, u32[]{:S(2)}, u32[]{:S(2)}) async-start(bf16[16,128,256]{2,1,0:T(8,128)(2,1)} %bitcast.43), calls=%async_computation.1 | async-start | bytes 2097152 | tf_op jit(solution)/shard_map/all_to_all | solution.py:84
  94.9 12.4 %all-to-all-done.1 = bf16[16,128,256]{2,1,0:T(8,128)(2,1)S(1)} async-done(((bf16[16,128,256]{2,1,0:T(8,128)(2,1)}), bf16[16,128,256]{2,1,0:T(8,128)(2,1)S(1)}, u32[]{:S(2)}, u32[]{:S(2)}) %all-to-all-start.1) | async-done | bytes 1048608 | tf_op jit(solution)/shard_map/all_to_all | solution.py:84
  107.4 0.7 copy.85
  108.0 0.6 multiply_reduce_fusion
  108.6 0.7 fusion.27
  109.3 1.2 convolution_convert_fusion
  110.6 0.3 copy.88
  110.9 1.0 pad_maximum_fusion.2
  111.9 43.1 %all-gather.4.cloned.1.call-done = bf16[640,4096]{1,0:T(8,128)(2,1)} async-done(((bf16[40,4096]{1,0:T(8,128)(2,1)}), bf16[640,4096]{1,0:T(8,128)(2,1)}) %all-gather.4.cloned.1.call-update) | async-done | bytes 5242896 | tf_op jit(solution)/shard_map/all_gather | solution.py:99
  155.0 95.8 %all-gather.6.cloned.1.call-done = bf16[48,28,4096]{2,1,0:T(8,128)(2,1)} async-done(((bf16[3,28,4096]{2,1,0:T(8,128)(2,1)}), bf16[48,28,4096]{2,1,0:T(8,128)(2,1)}) %all-gather.6.cloned.1.call-update) | async-done | bytes 11010064 | tf_op jit(solution)/shard_map/all_gather | solution.py:68
  250.8 10.7 %fusion.32 = f32[2,640,16,28]{1,3,0,2:T(8,128)S(1)} fusion(bf16[16,3,28,4096]{3,2,1,0:T(8,128)(2,1)} %bitcast.223, bf16[640,4096]{1,0:T(8,128)(2,1)} %all-gather.4.cloned.1.call-done), kind=kOutput, calls=%fused_computation.50 | convolution fusion | flops 4697620480 | bytes 18546688 | tf_op jit(solution)/shard_map/rd,jkud->krju/dot_general | solution.py:100
  261.6 7.5 %bitcast_convert_fusion = bf16[640,4096]{1,0:T(8,128)(2,1)} fusion(bf16[16,3,28,4096]{3,2,1,0:T(8,128)(2,1)} %bitcast.224, f32[2,640,16,28]{1,3,0,2:T(8,128)S(1)} %fusion.32), kind=kOutput, calls=%fused_computation.3 | convolution fusion | flops 2353152000 | bytes 11730944 | tf_op jit(solution)/shard_map/rju,jud->rd/dot_general | solution.py:104
  269.1 1.6 convert_element_type.134
  270.7 1.9 copy.95
  272.6 61.6 %reduce-scatter.2.cloned.1.call-done = bf16[40,4096]{1,0:T(8,128)(2,1)} async-done(((bf16[640,4096]{1,0:T(8,128)(2,1)}), bf16[40,4096]{1,0:T(8,128)(2,1)}) %reduce-scatter.2.cloned.1.call-update) | async-done | bytes 327696 | tf_op jit(solution)/shard_map/reduce_scatter | solution.py:107
  334.2 1.0 convert_element_type.129
  335.3 2.6 gather_fusion.2
  337.8 3.1 fusion.31
  (59 shorter events, 1.2 us)
Async XLA Ops:
  6.6 14.9 %copy-start.15 = (s32[1,16]{1,0:T(1,128)S(1)}, s32[1,16]{1,0:T(1,128)}, u32[]{:S(2)}) copy-start(s32[1,16]{1,0:T(1,128)} %param.12) | copy-start | bytes 196
  14.0 34.6 %all-to-all-start = ((bf16[16,128,512]{2,1,0:T(8,128)(2,1)}), bf16[16,128,512]{2,1,0:T(8,128)(2,1)S(1)}, u32[]{:S(2)}, u32[]{:S(2)}) async-start(bf16[16,128,512]{2,1,0:T(8,128)(2,1)} %pad_maximum_fusion), calls=%async_computation | async-start | bytes 4194304 | tf_op jit(solution)/shard_map/all_to_all | solution.py:76
  53.0 3.8 %copy-start.2 = (pred[512,2048]{0,1:T(8,128)(4,1)S(1)}, pred[512,2048]{0,1:T(8,128)(4,1)}, u32[]{:S(2)}) copy-start(pred[512,2048]{0,1:T(8,128)(4,1)} %get-tuple-element.13) | copy-start | bytes 3145732
  53.3 8.9 %copy-start.6 = (bf16[16,128,128]{2,1,0:T(8,128)(2,1)}, bf16[16,128,128]{2,1,0:T(8,128)(2,1)S(1)}, u32[]{:S(2)}) copy-start(bf16[16,128,128]{2,1,0:T(8,128)(2,1)S(1)} %get-tuple-element.11) | copy-start | bytes 1572868
  53.3 13.4 %copy-start.4 = (bf16[16,128,128]{2,1,0:T(8,128)(2,1)}, bf16[16,128,128]{2,1,0:T(8,128)(2,1)S(1)}, u32[]{:S(2)}) copy-start(bf16[16,128,128]{2,1,0:T(8,128)(2,1)S(1)} %get-tuple-element.12) | copy-start | bytes 1572868
  58.8 3.4 copy-start.1
  58.8 3.4 copy-start.9
  66.6 3.4 copy-start.3
  66.6 4.1 %copy-start = (pred[512,2048]{0,1:T(8,128)(4,1)S(1)}, pred[512,2048]{0,1:T(8,128)(4,1)}, u32[]{:S(2)}) copy-start(pred[512,2048]{0,1:T(8,128)(4,1)} %get-tuple-element.15) | copy-start | bytes 3145732
  66.6 4.1 %copy-start.7 = (bf16[16,128,128]{2,1,0:T(8,128)(2,1)S(1)}, bf16[16,128,128]{2,1,0:T(8,128)(2,1)}, u32[]{:S(2)}) copy-start(bf16[16,128,128]{2,1,0:T(8,128)(2,1)} %copy-done.6) | copy-start | bytes 1572868
  70.8 4.8 %copy-start.5 = (bf16[16,128,128]{2,1,0:T(8,128)(2,1)S(1)}, bf16[16,128,128]{2,1,0:T(8,128)(2,1)}, u32[]{:S(2)}) copy-start(bf16[16,128,128]{2,1,0:T(8,128)(2,1)} %copy-done.4) | copy-start | bytes 1572868
  83.4 2.7 copy-start.11
  83.5 2.7 copy-start.12
  83.5 2.7 copy-start.13
  83.5 11.0 %copy-start.16 = (s32[1,128,2]{1,2,0:T(2,128)S(1)}, s32[1,128,2]{1,2,0:T(2,128)}, u32[]{:S(2)}) copy-start(s32[1,128,2]{1,2,0:T(2,128)} %param.13) | copy-start | bytes 3076
  86.1 22.5 %copy-start.14 = (f32[4096]{0:T(1024)S(1)}, f32[4096]{0:T(1024)}, u32[]{:S(2)}) copy-start(f32[4096]{0:T(1024)} %param.15) | copy-start | bytes 49156
  86.1 24.5 %copy-start.8 = (bf16[2,28,4096]{2,0,1:T(2,128)(2,1)S(1)}, bf16[2,28,4096]{2,0,1:T(2,128)(2,1)}, u32[]{:S(2)}) copy-start(bf16[2,28,4096]{2,0,1:T(2,128)(2,1)} %param.16) | copy-start | bytes 1376260
  86.1 24.8 %copy-start.10 = (bf16[28,4096]{1,0:T(8,128)(2,1)S(1)}, bf16[28,4096]{1,0:T(8,128)(2,1)}, u32[]{:S(2)}) copy-start(bf16[28,4096]{1,0:T(8,128)(2,1)} %param.17) | copy-start | bytes 688132
  87.6 19.8 %all-to-all-start.1 = ((bf16[16,128,256]{2,1,0:T(8,128)(2,1)}), bf16[16,128,256]{2,1,0:T(8,128)(2,1)S(1)}, u32[]{:S(2)}, u32[]{:S(2)}) async-start(bf16[16,128,256]{2,1,0:T(8,128)(2,1)} %bitcast.43), calls=%async_computation.1 | async-start | bytes 2097152 | tf_op jit(solution)/shard_map/all_to_all | solution.py:84
  94.5 60.5 %all-gather.4.cloned.1.call-start = ((), (), s32[]{:S(2)}) async-start(), calls=%async_computation.3 | async-start | bytes 5570560 | tf_op jit(solution)/shard_map/all_gather | solution.py:99
  110.6 140.3 %all-gather.6.cloned.1.call-start = ((), (), s32[]{:S(2)}) async-start(), calls=%async_computation.5 | async-start | bytes 13369344 | tf_op jit(solution)/shard_map/all_gather | solution.py:68
  111.9 222.4 %reduce-scatter.2.cloned.1.call-start = ((), (), s32[]{:S(2)}) async-start(), calls=%async_computation.4 | async-start | bytes 5570560 | tf_op jit(solution)/shard_map/reduce_scatter | solution.py:107
  261.5 7.6 %copy-start.17 = (f32[1,128,2]{1,2,0:T(2,128)S(1)}, f32[1,128,2]{1,2,0:T(2,128)}, u32[]{:S(2)}) copy-start(f32[1,128,2]{1,2,0:T(2,128)} %param.14) | copy-start | bytes 3076
Sparse Core Ops, SparseCore 0:
  110.7 44.2 all-gather.3
  157.5 93.2 all-gather.5
  269.2 64.9 reduce-scatter.1

commit v2 on v1

--- a/solution.py
+++ b/solution.py
@@ -65,7 +65,7 @@
     kv_of_dest = (jnp.arange(seq_count) * per_dev) // (QH // KVH)
 
     weights_local = jnp.concatenate([w_in, w_down[None]], axis=0)[None]
-    weights_all = lax.all_gather(weights_local, "seq", axis=0, tiled=True)
+    weights_all = lax.all_gather(weights_local, "grp", axis=0, tiled=True)
 
     query_send = jnp.transpose(query_rows[0].reshape(tok_count, seq_count, feat), (1, 0, 2))
     key_send = jnp.transpose(key_rows[0].reshape(tok_count, KVH, HD)[:, kv_of_dest, :], (1, 0, 2))
@@ -96,7 +96,7 @@
     dispatched = jnp.dot(
         onehot.astype(jnp.bfloat16), normed, preferred_element_type=jnp.float32
     ).astype(jnp.bfloat16)
-    gathered = lax.all_gather(dispatched, "grp", axis=0, tiled=True)
+    gathered = lax.all_gather(dispatched, "seq", axis=0, tiled=True)
     gate_up = jnp.einsum(
         "rd,jkud->krju", gathered, weights_all[:, :2], preferred_element_type=jnp.float32
     )
@@ -105,7 +105,7 @@
         "rju,jud->rd", hidden, weights_all[:, 2], preferred_element_type=jnp.float32
     )
     returned = lax.psum_scatter(
-        terms.astype(jnp.bfloat16), "grp", scatter_dimension=0, tiled=True
+        terms.astype(jnp.bfloat16), "seq", scatter_dimension=0, tiled=True
     ).astype(jnp.float32)
     picked_rows = jnp.take(returned, jnp.clip(slot_index, 0, CAP - 1), axis=0)
     expert_out = jnp.where(routed[:, None], picked_rows, 0.0)

time: 348 us -> 366 us (1.052)
  waiting for transfers between devices: 236 us -> 254 us
    unnamed x3 -> x4, waiting for transfers between devices: 0.05 us -> 79.9 us
    reduce_scatter x1 -> x0, waiting for transfers between devices: 61.6 us -> none  [shards_body(): lax.psum_scatter(terms.astype(jnp.bfloat16), 'grp', scatter_dimension=0,...]
  transfers between devices with their start and end apart: 5 -> 5, of which waited for: 5 -> 5; matrix products, arithmetic and copies ran while one was open for 3% -> 2% of each run, Pallas kernels for 0% -> 0%
where the time goes in v2:
time: 366 us; the launch traced here: 365 us
  waiting for transfers between devices  254 us (69%)
  matrix products  42.8 us (12%)
  other arithmetic  22.1 us (6%)
  local copies, waits for them, and re-layouts  18.4 us (5%)
  starting transfers between devices  14.4 us (4%)
  between operations  13.5 us (4%)
    unnamed x4, waiting for transfers between devices  79.9 us
    all_gather x1, waiting for transfers between devices, shards_body(): weights_all = lax.all_gather(weights_local, 'grp', axis=0, tiled=True)  77.2 us
    all_gather x1, waiting for transfers between devices, shards_body(): gathered = lax.all_gather(dispatched, 'seq', axis=0, tiled=True)  61.1 us
    all_to_all x1, waiting for transfers between devices, shards_body(): packed_all = lax.all_to_all(packed, 'seq', 0, 0, tiled=False)  23.2 us
    dot_general x4, matrix products, attend(): jnp.einsum('gqt,td->qgd', weights.astype(jnp.bfloat16), value_all, prefer...  12.6 us
    all_to_all x1, waiting for transfers between devices, shards_body(): lax.all_to_all(attended.reshape(seq_count, tok_count, feat), 'seq', 0, 0,...  12.4 us
    dot_general x4, matrix products, attend(): jnp.einsum('qgd,td->gqt', query_tile, key_all, preferred_element_type=jnp...  10.8 us
    dot_general x1, matrix products, shards_body(): jnp.einsum('rd,jkud->krju', gathered, weights_all[:, :2], preferred_eleme...  10.7 us
  transfers between devices with their start and end apart: 5, of which 5 were waited for; matrix products, arithmetic and copies ran while one was open for 2% of the time, Pallas kernels for 0%

profile of v2, /device:TPU:2, one launch (start us, length us, event | category | flops | bytes accessed | tf_op | source)
XLA Modules:
  0.0 365.1 jit_solution(8176181039498538078)
XLA Ops:
  6.6 1.1 copy.71
  7.7 0.2 copy.72
  7.9 1.1 copy.73
  9.0 0.2 copy.74
  9.2 0.7 gather_fusion
  9.9 0.6 gather_fusion.1
  10.5 1.5 copy.96
  12.0 0.3 copy.114
  12.3 1.6 pad_maximum_fusion
  14.0 7.5 %all-to-all-start = ((bf16[16,128,512]{2,1,0:T(8,128)(2,1)}), bf16[16,128,512]{2,1,0:T(8,128)(2,1)S(1)}, u32[]{:S(2)}, u32[]{:S(2)}) async-start(bf16[16,128,512]{2,1,0:T(8,128)(2,1)} %pad_maximum_fusion), calls=%async_computation | async-start | bytes 4194304 | tf_op jit(solution)/shard_map/all_to_all | solution.py:76
  21.7 3.7 %broadcast_compare_fusion.3 = (pred[512,2048]{0,1:T(8,128)(4,1)}, pred[512,2048]{0,1:T(8,128)(4,1)}, pred[512,2048]{0,1:T(8,128)(4,1)}, pred[512,2048]{0,1:T(8,128)(4,1)S(1)}) fusion(s32[512]{0:T(512)S(1)} %get-tuple-element.32, s32[2048]{0:T(1024)S(1)} %broadcast_bitcast_fusion, s32[512]{0:T(512)S(1)} %get-tuple-element.31, s32[512]{0:T(512)S(1)} %get-tuple-element.30, ...), kind=kLoop, calls=%fused_computation.49 | loop fusion | flops 4194304 | bytes 4210688 | tf_op jit(solution)/shard_map/eq | solution.py:30
  25.4 23.2 %all-to-all-done = bf16[16,128,512]{2,1,0:T(8,128)(2,1)S(1)} async-done(((bf16[16,128,512]{2,1,0:T(8,128)(2,1)}), bf16[16,128,512]{2,1,0:T(8,128)(2,1)S(1)}, u32[]{:S(2)}, u32[]{:S(2)}) %all-to-all-start) | async-done | bytes 2097184 | tf_op jit(solution)/shard_map/all_to_all | solution.py:76
  48.6 0.9 fusion.98
  49.5 1.7 slice.84
  51.3 1.7 slice.88
  53.0 0.3 fusion.99
  53.3 3.5 fusion.8
  56.8 2.0 fusion
  58.9 3.3 fusion.69
  62.2 2.2 fusion.9
  64.4 2.2 fusion.2
  66.7 3.3 fusion.63
  70.0 0.8 slice.92
  70.8 2.8 fusion.10
  73.6 2.0 fusion.4
  75.6 3.3 fusion.57
  79.0 2.2 fusion.11
  81.2 2.2 fusion.6
  83.5 2.6 fusion.51
  86.3 1.3 copy.84
  87.6 6.8 %all-to-all-start.1 = ((bf16[16,128,256]{2,1,0:T(8,128)(2,1)}), bf16[16,128,256]{2,1,0:T(8,128)(2,1)S(1)}, u32[]{:S(2)}, u32[]{:S(2)}) async-start(bf16[16,128,256]{2,1,0:T(8,128)(2,1)} %bitcast.43), calls=%async_computation.1 | async-start | bytes 2097152 | tf_op jit(solution)/shard_map/all_to_all | solution.py:84
  94.9 12.4 %all-to-all-done.1 = bf16[16,128,256]{2,1,0:T(8,128)(2,1)S(1)} async-done(((bf16[16,128,256]{2,1,0:T(8,128)(2,1)}), bf16[16,128,256]{2,1,0:T(8,128)(2,1)S(1)}, u32[]{:S(2)}, u32[]{:S(2)}) %all-to-all-start.1) | async-done | bytes 1048608 | tf_op jit(solution)/shard_map/all_to_all | solution.py:84
  107.4 0.7 copy.85
  108.0 0.6 multiply_reduce_fusion
  108.6 0.7 fusion.27
  109.3 1.2 convolution_convert_fusion
  110.6 0.3 copy.88
  110.9 1.0 pad_maximum_fusion.2
  111.9 61.1 %all-gather.4.cloned.1.call-done = bf16[640,4096]{1,0:T(8,128)(2,1)} async-done(((bf16[40,4096]{1,0:T(8,128)(2,1)}), bf16[640,4096]{1,0:T(8,128)(2,1)}) %all-gather.4.cloned.1.call-update) | async-done | bytes 5242896 | tf_op jit(solution)/shard_map/all_gather | solution.py:99
  173.1 77.2 %all-gather.6.cloned.1.call-done = bf16[48,28,4096]{2,1,0:T(8,128)(2,1)} async-done(((bf16[3,28,4096]{2,1,0:T(8,128)(2,1)}), bf16[48,28,4096]{2,1,0:T(8,128)(2,1)}) %all-gather.6.cloned.1.call-update) | async-done | bytes 11010064 | tf_op jit(solution)/shard_map/all_gather | solution.py:68
  250.2 10.7 %fusion.32 = f32[2,640,16,28]{1,3,0,2:T(8,128)S(1)} fusion(bf16[16,3,28,4096]{3,2,1,0:T(8,128)(2,1)} %bitcast.224, bf16[640,4096]{1,0:T(8,128)(2,1)} %all-gather.4.cloned.1.call-done), kind=kOutput, calls=%fused_computation.50 | convolution fusion | flops 4697620480 | bytes 18546688 | tf_op jit(solution)/shard_map/rd,jkud->krju/dot_general | solution.py:100
  261.0 7.5 %bitcast_convert_fusion = bf16[640,4096]{1,0:T(8,128)(2,1)} fusion(bf16[16,3,28,4096]{3,2,1,0:T(8,128)(2,1)} %bitcast.225, f32[2,640,16,28]{1,3,0,2:T(8,128)S(1)} %fusion.32), kind=kOutput, calls=%fused_computation.3 | convolution fusion | flops 2353152000 | bytes 11730944 | tf_op jit(solution)/shard_map/rju,jud->rd/dot_general | solution.py:104
  268.6 1.6 convert_element_type.134
  270.1 1.9 copy.95
  272.1 79.9 %reduce-scatter.4.cloned.1.call-done = bf16[40,4096]{1,0:T(8,128)(2,1)} async-done(((bf16[640,4096]{1,0:T(8,128)(2,1)}), bf16[40,4096]{1,0:T(8,128)(2,1)}) %reduce-scatter.4.cloned.1.call-update) | async-done | bytes 327696
  351.9 1.0 convert_element_type.129
  353.0 2.6 gather_fusion.2
  355.5 3.1 fusion.31
  (59 shorter events, 1.2 us)
Async XLA Ops:
  6.6 14.9 %copy-start.15 = (s32[1,16]{1,0:T(1,128)S(1)}, s32[1,16]{1,0:T(1,128)}, u32[]{:S(2)}) copy-start(s32[1,16]{1,0:T(1,128)} %param.12) | copy-start | bytes 196
  14.0 34.6 %all-to-all-start = ((bf16[16,128,512]{2,1,0:T(8,128)(2,1)}), bf16[16,128,512]{2,1,0:T(8,128)(2,1)S(1)}, u32[]{:S(2)}, u32[]{:S(2)}) async-start(bf16[16,128,512]{2,1,0:T(8,128)(2,1)} %pad_maximum_fusion), calls=%async_computation | async-start | bytes 4194304 | tf_op jit(solution)/shard_map/all_to_all | solution.py:76
  53.0 3.8 %copy-start.2 = (pred[512,2048]{0,1:T(8,128)(4,1)S(1)}, pred[512,2048]{0,1:T(8,128)(4,1)}, u32[]{:S(2)}) copy-start(pred[512,2048]{0,1:T(8,128)(4,1)} %get-tuple-element.13) | copy-start | bytes 3145732
  53.3 8.9 %copy-start.6 = (bf16[16,128,128]{2,1,0:T(8,128)(2,1)}, bf16[16,128,128]{2,1,0:T(8,128)(2,1)S(1)}, u32[]{:S(2)}) copy-start(bf16[16,128,128]{2,1,0:T(8,128)(2,1)S(1)} %get-tuple-element.11) | copy-start | bytes 1572868
  53.3 13.4 %copy-start.4 = (bf16[16,128,128]{2,1,0:T(8,128)(2,1)}, bf16[16,128,128]{2,1,0:T(8,128)(2,1)S(1)}, u32[]{:S(2)}) copy-start(bf16[16,128,128]{2,1,0:T(8,128)(2,1)S(1)} %get-tuple-element.12) | copy-start | bytes 1572868
  58.8 3.4 copy-start.1
  58.8 3.4 copy-start.9
  66.6 3.4 copy-start.3
  66.6 4.1 %copy-start = (pred[512,2048]{0,1:T(8,128)(4,1)S(1)}, pred[512,2048]{0,1:T(8,128)(4,1)}, u32[]{:S(2)}) copy-start(pred[512,2048]{0,1:T(8,128)(4,1)} %get-tuple-element.15) | copy-start | bytes 3145732
  66.6 4.1 %copy-start.7 = (bf16[16,128,128]{2,1,0:T(8,128)(2,1)S(1)}, bf16[16,128,128]{2,1,0:T(8,128)(2,1)}, u32[]{:S(2)}) copy-start(bf16[16,128,128]{2,1,0:T(8,128)(2,1)} %copy-done.6) | copy-start | bytes 1572868
  70.8 4.8 %copy-start.5 = (bf16[16,128,128]{2,1,0:T(8,128)(2,1)S(1)}, bf16[16,128,128]{2,1,0:T(8,128)(2,1)}, u32[]{:S(2)}) copy-start(bf16[16,128,128]{2,1,0:T(8,128)(2,1)} %copy-done.4) | copy-start | bytes 1572868
  83.4 2.7 copy-start.11
  83.5 2.7 copy-start.12
  83.5 2.7 copy-start.13
  83.5 11.0 %copy-start.16 = (s32[1,128,2]{1,2,0:T(2,128)S(1)}, s32[1,128,2]{1,2,0:T(2,128)}, u32[]{:S(2)}) copy-start(s32[1,128,2]{1,2,0:T(2,128)} %param.13) | copy-start | bytes 3076
  86.1 22.5 %copy-start.14 = (f32[4096]{0:T(1024)S(1)}, f32[4096]{0:T(1024)}, u32[]{:S(2)}) copy-start(f32[4096]{0:T(1024)} %param.15) | copy-start | bytes 49156
  86.1 24.5 %copy-start.8 = (bf16[2,28,4096]{2,0,1:T(2,128)(2,1)S(1)}, bf16[2,28,4096]{2,0,1:T(2,128)(2,1)}, u32[]{:S(2)}) copy-start(bf16[2,28,4096]{2,0,1:T(2,128)(2,1)} %param.16) | copy-start | bytes 1376260
  86.1 24.8 %copy-start.10 = (bf16[28,4096]{1,0:T(8,128)(2,1)S(1)}, bf16[28,4096]{1,0:T(8,128)(2,1)}, u32[]{:S(2)}) copy-start(bf16[28,4096]{1,0:T(8,128)(2,1)} %param.17) | copy-start | bytes 688132
  87.6 19.8 %all-to-all-start.1 = ((bf16[16,128,256]{2,1,0:T(8,128)(2,1)}), bf16[16,128,256]{2,1,0:T(8,128)(2,1)S(1)}, u32[]{:S(2)}, u32[]{:S(2)}) async-start(bf16[16,128,256]{2,1,0:T(8,128)(2,1)} %bitcast.43), calls=%async_computation.1 | async-start | bytes 2097152 | tf_op jit(solution)/shard_map/all_to_all | solution.py:84
  94.5 78.6 %all-gather.4.cloned.1.call-start = ((), (), s32[]{:S(2)}) async-start(), calls=%async_computation.3 | async-start | bytes 5570560 | tf_op jit(solution)/shard_map/all_gather | solution.py:99
  110.6 139.7 %all-gather.6.cloned.1.call-start = ((), (), s32[]{:S(2)}) async-start(), calls=%async_computation.4 | async-start | bytes 13369344 | tf_op jit(solution)/shard_map/all_gather | solution.py:68
  111.9 240.1 %reduce-scatter.4.cloned.1.call-start = ((), (), s32[]{:S(2)}) async-start(), calls=%async_computation.5 | async-start | bytes 5570560
  261.0 7.6 %copy-start.17 = (f32[1,128,2]{1,2,0:T(2,128)S(1)}, f32[1,128,2]{1,2,0:T(2,128)}, u32[]{:S(2)}) copy-start(f32[1,128,2]{1,2,0:T(2,128)} %param.14) | copy-start | bytes 3076
Sparse Core Ops, SparseCore 0:
  110.7 62.3 all-gather.3
  174.9 75.3 all-gather.5
  268.6 83.2 reduce-scatter.3

commit v3 on v2

--- a/solution.py
+++ b/solution.py
@@ -104,9 +104,10 @@
     terms = jnp.einsum(
         "rju,jud->rd", hidden, weights_all[:, 2], preferred_element_type=jnp.float32
     )
-    returned = lax.psum_scatter(
-        terms.astype(jnp.bfloat16), "seq", scatter_dimension=0, tiled=True
-    ).astype(jnp.float32)
+    partials = lax.all_to_all(
+        terms.astype(jnp.bfloat16).reshape(seq_count, CAP, -1), "seq", 0, 0, tiled=False
+    )
+    returned = jnp.sum(partials.astype(jnp.float32), axis=0)
     picked_rows = jnp.take(returned, jnp.clip(slot_index, 0, CAP - 1), axis=0)
     expert_out = jnp.where(routed[:, None], picked_rows, 0.0)
     layer_out = attn_float + gate_share[:, None] * expert_out

time: 366 us -> 376 us (1.027)
  the two profiles are of different devices: /device:TPU:2 before, /device:TPU:28 now
where the time goes in v3:
time: 376 us; the launch traced here: 375 us
  waiting for transfers between devices  253 us (67%)
  matrix products  42.9 us (11%)
  other arithmetic  24.6 us (7%)
  starting transfers between devices  21.9 us (6%)
  local copies, waits for them, and re-layouts  18.6 us (5%)
  between operations  13.8 us (4%)
    all_to_all x1, waiting for transfers between devices, shards_body(): lax.all_to_all(terms.astype(jnp.bfloat16).reshape(seq_count, CAP, -1), 's...  79.7 us
    all_gather x1, waiting for transfers between devices, shards_body(): weights_all = lax.all_gather(weights_local, 'grp', axis=0, tiled=True)  78.8 us
    all_gather x1, waiting for transfers between devices, shards_body(): gathered = lax.all_gather(dispatched, 'seq', axis=0, tiled=True)  61.4 us
    all_to_all x1, waiting for transfers between devices, shards_body(): packed_all = lax.all_to_all(packed, 'seq', 0, 0, tiled=False)  22.7 us
    dot_general x4, matrix products, attend(): jnp.einsum('gqt,td->qgd', weights.astype(jnp.bfloat16), value_all, prefer...  12.6 us
    dot_general x4, matrix products, attend(): jnp.einsum('qgd,td->gqt', query_tile, key_all, preferred_element_type=jnp...  10.9 us
    dot_general x1, matrix products, shards_body(): jnp.einsum('rd,jkud->krju', gathered, weights_all[:, :2], preferred_eleme...  10.7 us
    all_to_all x1, waiting for transfers between devices, shards_body(): lax.all_to_all(attended.reshape(seq_count, tok_count, feat), 'seq', 0, 0,...  10.7 us
  transfers between devices with their start and end apart: 5, of which 5 were waited for; matrix products, arithmetic and copies ran while one was open for 2% of the time, Pallas kernels for 0%

profile of v3, /device:TPU:28, one launch (start us, length us, event | category | flops | bytes accessed | tf_op | source)
XLA Modules:
  0.0 375.1 jit_solution(2309676355930531611)
XLA Ops:
  6.6 1.1 copy.71
  7.9 1.1 copy.73
  9.0 0.2 copy.74
  9.2 0.7 gather_fusion
  9.9 0.6 gather_fusion.1
  10.5 1.5 copy.96
  12.0 0.3 copy.114
  12.3 1.6 pad_maximum_fusion
  14.0 7.1 %all-to-all-start = ((bf16[16,128,512]{2,1,0:T(8,128)(2,1)}), bf16[16,128,512]{2,1,0:T(8,128)(2,1)S(1)}, u32[]{:S(2)}, u32[]{:S(2)}) async-start(bf16[16,128,512]{2,1,0:T(8,128)(2,1)} %pad_maximum_fusion), calls=%async_computation | async-start | bytes 4194304 | tf_op jit(solution)/shard_map/all_to_all | solution.py:76
  21.4 3.7 broadcast_compare_fusion.3
  25.0 22.7 %all-to-all-done = bf16[16,128,512]{2,1,0:T(8,128)(2,1)S(1)} async-done(((bf16[16,128,512]{2,1,0:T(8,128)(2,1)}), bf16[16,128,512]{2,1,0:T(8,128)(2,1)S(1)}, u32[]{:S(2)}, u32[]{:S(2)}) %all-to-all-start) | async-done | bytes 2097184 | tf_op jit(solution)/shard_map/all_to_all | solution.py:76
  47.7 0.9 fusion.98
  48.6 1.7 slice.84
  50.4 1.7 slice.88
  52.1 0.3 fusion.99
  52.4 3.5 fusion.8
  55.9 2.0 fusion
  58.0 3.3 fusion.69
  61.3 2.2 fusion.9
  63.5 2.2 fusion.2
  65.7 3.3 fusion.63
  69.0 1.0 slice.92
  70.1 2.9 fusion.10
  73.0 2.0 fusion.4
  75.0 3.3 fusion.57
  78.4 2.2 fusion.11
  80.7 2.2 fusion.6
  82.9 2.6 fusion.51
  85.8 1.3 copy.84
  87.1 7.4 %all-to-all-start.1 = ((bf16[16,128,256]{2,1,0:T(8,128)(2,1)}), bf16[16,128,256]{2,1,0:T(8,128)(2,1)S(1)}, u32[]{:S(2)}, u32[]{:S(2)}) async-start(bf16[16,128,256]{2,1,0:T(8,128)(2,1)} %bitcast.43), calls=%async_computation.1 | async-start | bytes 2097152 | tf_op jit(solution)/shard_map/all_to_all | solution.py:84
  94.9 10.7 %all-to-all-done.1 = bf16[16,128,256]{2,1,0:T(8,128)(2,1)S(1)} async-done(((bf16[16,128,256]{2,1,0:T(8,128)(2,1)}), bf16[16,128,256]{2,1,0:T(8,128)(2,1)S(1)}, u32[]{:S(2)}, u32[]{:S(2)}) %all-to-all-start.1) | async-done | bytes 1048608 | tf_op jit(solution)/shard_map/all_to_all | solution.py:84
  105.6 0.7 copy.85
  106.3 0.6 multiply_reduce_fusion
  106.8 0.7 fusion.27
  107.5 1.2 convolution_convert_fusion
  108.8 0.3 copy.88
  109.1 1.0 pad_maximum_fusion.2
  110.1 61.4 %all-gather.4.cloned.1.call-done = bf16[640,4096]{1,0:T(8,128)(2,1)} async-done(((bf16[40,4096]{1,0:T(8,128)(2,1)}), bf16[640,4096]{1,0:T(8,128)(2,1)}) %all-gather.4.cloned.1.call-update) | async-done | bytes 5242896 | tf_op jit(solution)/shard_map/all_gather | solution.py:99
  171.5 78.8 %all-gather.6.cloned.1.call-done = bf16[48,28,4096]{2,1,0:T(8,128)(2,1)} async-done(((bf16[3,28,4096]{2,1,0:T(8,128)(2,1)}), bf16[48,28,4096]{2,1,0:T(8,128)(2,1)}) %all-gather.6.cloned.1.call-update) | async-done | bytes 11010064 | tf_op jit(solution)/shard_map/all_gather | solution.py:68
  250.3 10.7 %fusion.32 = f32[2,640,16,28]{1,3,0,2:T(8,128)S(1)} fusion(bf16[16,3,28,4096]{3,2,1,0:T(8,128)(2,1)} %bitcast.225, bf16[640,4096]{1,0:T(8,128)(2,1)} %all-gather.4.cloned.1.call-done), kind=kOutput, calls=%fused_computation.51 | convolution fusion | flops 4697620480 | bytes 18546688 | tf_op jit(solution)/shard_map/rd,jkud->krju/dot_general | solution.py:100
  261.0 7.5 %bitcast_convert_fusion = bf16[640,4096]{1,0:T(8,128)(2,1)} fusion(bf16[16,3,28,4096]{3,2,1,0:T(8,128)(2,1)} %bitcast.226, f32[2,640,16,28]{1,3,0,2:T(8,128)S(1)} %fusion.32), kind=kOutput, calls=%fused_computation.3 | convolution fusion | flops 2353152000 | bytes 11730944 | tf_op jit(solution)/shard_map/rju,jud->rd/dot_general | solution.py:104
  268.5 7.3 %all-to-all-start.2 = ((bf16[16,40,4096]{2,1,0:T(8,128)(2,1)}), bf16[16,40,4096]{2,1,0:T(8,128)(2,1)}, u32[]{:S(2)}, u32[]{:S(2)}) async-start(bf16[16,40,4096]{2,1,0:T(8,128)(2,1)} %bitcast.201), calls=%async_computation.2 | async-start | bytes 10485760 | tf_op jit(solution)/shard_map/all_to_all | solution.py:107
  275.9 1.6 convert_element_type.134
  277.5 1.9 copy.95
  279.4 79.7 %all-to-all-done.2 = bf16[16,40,4096]{2,1,0:T(8,128)(2,1)} async-done(((bf16[16,40,4096]{2,1,0:T(8,128)(2,1)}), bf16[16,40,4096]{2,1,0:T(8,128)(2,1)}, u32[]{:S(2)}, u32[]{:S(2)}) %all-to-all-start.2) | async-done | bytes 5242912 | tf_op jit(solution)/shard_map/all_to_all | solution.py:107
  359.1 3.5 convert_reduce_fusion
  362.6 2.6 gather_fusion.2
  365.2 3.1 fusion.31
  (56 shorter events, 1.3 us)
Async XLA Ops:
  6.6 14.5 %copy-start.14 = (s32[1,16]{1,0:T(1,128)S(1)}, s32[1,16]{1,0:T(1,128)}, u32[]{:S(2)}) copy-start(s32[1,16]{1,0:T(1,128)} %param.12) | copy-start | bytes 196
  14.0 33.7 %all-to-all-start = ((bf16[16,128,512]{2,1,0:T(8,128)(2,1)}), bf16[16,128,512]{2,1,0:T(8,128)(2,1)S(1)}, u32[]{:S(2)}, u32[]{:S(2)}) async-start(bf16[16,128,512]{2,1,0:T(8,128)(2,1)} %pad_maximum_fusion), calls=%async_computation | async-start | bytes 4194304 | tf_op jit(solution)/shard_map/all_to_all | solution.py:76
  52.1 3.8 %copy-start.2 = (pred[512,2048]{0,1:T(8,128)(4,1)S(1)}, pred[512,2048]{0,1:T(8,128)(4,1)}, u32[]{:S(2)}) copy-start(pred[512,2048]{0,1:T(8,128)(4,1)} %get-tuple-element.13) | copy-start | bytes 3145732
  52.4 8.9 %copy-start.5 = (bf16[16,128,128]{2,1,0:T(8,128)(2,1)}, bf16[16,128,128]{2,1,0:T(8,128)(2,1)S(1)}, u32[]{:S(2)}) copy-start(bf16[16,128,128]{2,1,0:T(8,128)(2,1)S(1)} %get-tuple-element.11) | copy-start | bytes 1572868
  52.4 13.3 %copy-start.3 = (bf16[16,128,128]{2,1,0:T(8,128)(2,1)}, bf16[16,128,128]{2,1,0:T(8,128)(2,1)S(1)}, u32[]{:S(2)}) copy-start(bf16[16,128,128]{2,1,0:T(8,128)(2,1)S(1)} %get-tuple-element.12) | copy-start | bytes 1572868
  57.9 3.3 copy-start.1
  57.9 3.3 copy-start.8
  65.7 4.4 %copy-start = (pred[512,2048]{0,1:T(8,128)(4,1)S(1)}, pred[512,2048]{0,1:T(8,128)(4,1)}, u32[]{:S(2)}) copy-start(pred[512,2048]{0,1:T(8,128)(4,1)} %get-tuple-element.15) | copy-start | bytes 3145732
  70.1 5.0 %copy-start.4 = (bf16[16,128,128]{2,1,0:T(8,128)(2,1)S(1)}, bf16[16,128,128]{2,1,0:T(8,128)(2,1)}, u32[]{:S(2)}) copy-start(bf16[16,128,128]{2,1,0:T(8,128)(2,1)} %copy-done.3) | copy-start | bytes 1572868
  75.0 3.4 copy-start.6
  82.9 2.7 copy-start.10
  82.9 2.7 copy-start.11
  82.9 2.7 copy-start.12
  82.9 11.6 %copy-start.15 = (s32[1,128,2]{1,2,0:T(2,128)S(1)}, s32[1,128,2]{1,2,0:T(2,128)}, u32[]{:S(2)}) copy-start(s32[1,128,2]{1,2,0:T(2,128)} %param.13) | copy-start | bytes 3076
  85.6 21.3 %copy-start.13 = (f32[4096]{0:T(1024)S(1)}, f32[4096]{0:T(1024)}, u32[]{:S(2)}) copy-start(f32[4096]{0:T(1024)} %param.15) | copy-start | bytes 49156
  85.6 23.2 %copy-start.7 = (bf16[2,28,4096]{2,0,1:T(2,128)(2,1)S(1)}, bf16[2,28,4096]{2,0,1:T(2,128)(2,1)}, u32[]{:S(2)}) copy-start(bf16[2,28,4096]{2,0,1:T(2,128)(2,1)} %param.16) | copy-start | bytes 1376260
  85.6 23.5 %copy-start.9 = (bf16[28,4096]{1,0:T(8,128)(2,1)S(1)}, bf16[28,4096]{1,0:T(8,128)(2,1)}, u32[]{:S(2)}) copy-start(bf16[28,4096]{1,0:T(8,128)(2,1)} %param.17) | copy-start | bytes 688132
  87.1 18.5 %all-to-all-start.1 = ((bf16[16,128,256]{2,1,0:T(8,128)(2,1)}), bf16[16,128,256]{2,1,0:T(8,128)(2,1)S(1)}, u32[]{:S(2)}, u32[]{:S(2)}) async-start(bf16[16,128,256]{2,1,0:T(8,128)(2,1)} %bitcast.43), calls=%async_computation.1 | async-start | bytes 2097152 | tf_op jit(solution)/shard_map/all_to_all | solution.py:84
  94.5 77.1 %all-gather.4.cloned.1.call-start = ((), (), s32[]{:S(2)}) async-start(), calls=%async_computation.3 | async-start | bytes 5570560 | tf_op jit(solution)/shard_map/all_gather | solution.py:99
  108.8 141.5 %all-gather.6.cloned.1.call-start = ((), (), s32[]{:S(2)}) async-start(), calls=%async_computation.4 | async-start | bytes 13369344 | tf_op jit(solution)/shard_map/all_gather | solution.py:68
  268.5 7.3 %copy-start.16 = (f32[1,128,2]{1,2,0:T(2,128)S(1)}, f32[1,128,2]{1,2,0:T(2,128)}, u32[]{:S(2)}) copy-start(f32[1,128,2]{1,2,0:T(2,128)} %param.14) | copy-start | bytes 3076
  268.5 90.6 %all-to-all-start.2 = ((bf16[16,40,4096]{2,1,0:T(8,128)(2,1)}), bf16[16,40,4096]{2,1,0:T(8,128)(2,1)}, u32[]{:S(2)}, u32[]{:S(2)}) async-start(bf16[16,40,4096]{2,1,0:T(8,128)(2,1)} %bitcast.201), calls=%async_computation.2 | async-start | bytes 10485760 | tf_op jit(solution)/shard_map/all_to_all | solution.py:107
Sparse Core Ops, SparseCore 0:
  108.9 62.5 all-gather.3
  173.4 76.8 all-gather.5

commit v4 on v1

--- a/solution.py
+++ b/solution.py
@@ -97,16 +97,26 @@
         onehot.astype(jnp.bfloat16), normed, preferred_element_type=jnp.float32
     ).astype(jnp.bfloat16)
     gathered = lax.all_gather(dispatched, "grp", axis=0, tiled=True)
-    gate_up = jnp.einsum(
-        "rd,jkud->krju", gathered, weights_all[:, :2], preferred_element_type=jnp.float32
-    )
-    hidden = (jax.nn.silu(gate_up[0]) * gate_up[1]).astype(jnp.bfloat16)
-    terms = jnp.einsum(
-        "rju,jud->rd", hidden, weights_all[:, 2], preferred_element_type=jnp.float32
-    )
-    returned = lax.psum_scatter(
-        terms.astype(jnp.bfloat16), "grp", scatter_dimension=0, tiled=True
-    ).astype(jnp.float32)
+    grp_count = gathered.shape[0] // CAP
+    by_source = gathered.reshape(grp_count, CAP, -1)
+    cuts = (0, 24, CAP)
+    pieces = []
+    for part in range(2):
+        lo, hi = cuts[part], cuts[part + 1]
+        rows = by_source[:, lo:hi].reshape(grp_count * (hi - lo), -1)
+        gate_up = jnp.einsum(
+            "rd,jkud->krju", rows, weights_all[:, :2], preferred_element_type=jnp.float32
+        )
+        hidden = (jax.nn.silu(gate_up[0]) * gate_up[1]).astype(jnp.bfloat16)
+        terms = jnp.einsum(
+            "rju,jud->rd", hidden, weights_all[:, 2], preferred_element_type=jnp.float32
+        )
+        pieces.append(
+            lax.psum_scatter(
+                terms.astype(jnp.bfloat16), "grp", scatter_dimension=0, tiled=True
+            )
+        )
+    returned = jnp.concatenate(pieces, axis=0).astype(jnp.float32)
     picked_rows = jnp.take(returned, jnp.clip(slot_index, 0, CAP - 1), axis=0)
     expert_out = jnp.where(routed[:, None], picked_rows, 0.0)
     layer_out = attn_float + gate_share[:, None] * expert_out

time: 348 us -> 398 us (1.14)
  waiting for transfers between devices: 236 us -> 276 us
  matrix products: 42.8 us -> 48.3 us
  local copies, waits for them, and re-layouts: 18.4 us -> 22.6 us
    reduce_scatter x1 -> x2, waiting for transfers between devices: 61.6 us -> 104 us  [shards_body(): lax.psum_scatter(terms.astype(jnp.bfloat16), 'grp', scatter_dimension=0,...]
    dot_general x1 -> x2, matrix products: 7.51 us -> 10.7 us  [shards_body(): jnp.einsum('rju,jud->rd', hidden, weights_all[:, 2], preferred_element_ty...]
    dot_general x1 -> x2, matrix products: 10.7 us -> 13 us  [shards_body(): jnp.einsum('rd,jkud->krju', rows, weights_all[:, :2], preferred_element_t...]
  transfers between devices with their start and end apart: 5 -> 6, of which waited for: 5 -> 6; matrix products, arithmetic and copies ran while one was open for 3% -> 7% of each run, Pallas kernels for 0% -> 0%
where the time goes in v4:
time: 398 us; the launch traced here: 397 us
  waiting for transfers between devices  276 us (69%)
  matrix products  48.3 us (12%)
  local copies, waits for them, and re-layouts  22.6 us (6%)
  other arithmetic  22 us (6%)
  starting transfers between devices  14.5 us (4%)
  between operations  13.6 us (3%)
    reduce_scatter x2, waiting for transfers between devices, shards_body(): lax.psum_scatter(terms.astype(jnp.bfloat16), 'grp', scatter_dimension=0,...  104 us
    all_gather x1, waiting for transfers between devices, shards_body(): weights_all = lax.all_gather(weights_local, 'seq', axis=0, tiled=True)  94.1 us
    all_gather x1, waiting for transfers between devices, shards_body(): gathered = lax.all_gather(dispatched, 'grp', axis=0, tiled=True)  43.1 us
    all_to_all x1, waiting for transfers between devices, shards_body(): packed_all = lax.all_to_all(packed, 'seq', 0, 0, tiled=False)  23.2 us
    dot_general x2, matrix products, shards_body(): jnp.einsum('rd,jkud->krju', rows, weights_all[:, :2], preferred_element_t...  13 us
    dot_general x4, matrix products, attend(): jnp.einsum('gqt,td->qgd', weights.astype(jnp.bfloat16), value_all, prefer...  12.6 us
    all_to_all x1, waiting for transfers between devices, shards_body(): lax.all_to_all(attended.reshape(seq_count, tok_count, feat), 'seq', 0, 0,...  12.4 us
    dot_general x4, matrix products, attend(): jnp.einsum('qgd,td->gqt', query_tile, key_all, preferred_element_type=jnp...  10.9 us
  transfers between devices with their start and end apart: 6, of which 6 were waited for; matrix products, arithmetic and copies ran while one was open for 7% of the time, Pallas kernels for 0%

profile of v4, /device:TPU:2, one launch (start us, length us, event | category | flops | bytes accessed | tf_op | source)
XLA Modules:
  0.0 397.5 jit_solution(5740649955896220147)
XLA Ops:
  6.6 1.1 copy.73
  7.9 1.1 copy.71
  9.2 0.7 gather_fusion.1
  9.9 0.6 gather_fusion
  10.5 1.5 copy.97
  12.3 1.6 pad_maximum_fusion
  14.0 7.5 %all-to-all-start = ((bf16[16,128,512]{2,1,0:T(8,128)(2,1)}), bf16[16,128,512]{2,1,0:T(8,128)(2,1)S(1)}, u32[]{:S(2)}, u32[]{:S(2)}) async-start(bf16[16,128,512]{2,1,0:T(8,128)(2,1)} %pad_maximum_fusion), calls=%async_computation | async-start | bytes 4194304 | tf_op jit(solution)/shard_map/all_to_all | solution.py:76
  21.7 3.7 broadcast_compare_fusion.3
  25.4 23.2 %all-to-all-done = bf16[16,128,512]{2,1,0:T(8,128)(2,1)S(1)} async-done(((bf16[16,128,512]{2,1,0:T(8,128)(2,1)}), bf16[16,128,512]{2,1,0:T(8,128)(2,1)S(1)}, u32[]{:S(2)}, u32[]{:S(2)}) %all-to-all-start) | async-done | bytes 2097184 | tf_op jit(solution)/shard_map/all_to_all | solution.py:76
  48.6 0.9 fusion.98
  49.6 1.7 slice.110
  51.3 1.7 slice.106
  53.3 3.5 fusion.11
  56.8 2.0 fusion.6
  58.9 3.3 fusion.46
  62.2 2.2 fusion.10
  64.4 2.2 fusion.4
  66.6 3.3 fusion.52
  69.9 1.0 slice.102
  71.0 2.9 fusion.9
  73.9 2.0 fusion.2
  75.9 3.3 fusion.58
  79.3 2.2 fusion.8
  81.6 2.2 fusion
  83.8 2.6 fusion.64
  86.7 1.3 copy.84
  88.0 6.8 %all-to-all-start.1 = ((bf16[16,128,256]{2,1,0:T(8,128)(2,1)}), bf16[16,128,256]{2,1,0:T(8,128)(2,1)S(1)}, u32[]{:S(2)}, u32[]{:S(2)}) async-start(bf16[16,128,256]{2,1,0:T(8,128)(2,1)} %bitcast.43), calls=%async_computation.1 | async-start | bytes 2097152 | tf_op jit(solution)/shard_map/all_to_all | solution.py:84
  95.3 12.4 %all-to-all-done.1 = bf16[16,128,256]{2,1,0:T(8,128)(2,1)S(1)} async-done(((bf16[16,128,256]{2,1,0:T(8,128)(2,1)}), bf16[16,128,256]{2,1,0:T(8,128)(2,1)S(1)}, u32[]{:S(2)}, u32[]{:S(2)}) %all-to-all-start.1) | async-done | bytes 1048608 | tf_op jit(solution)/shard_map/all_to_all | solution.py:84
  107.8 0.7 copy.85
  108.4 0.6 multiply_reduce_fusion
  109.0 0.7 fusion.26
  109.7 1.2 convolution_convert_fusion
  111.3 1.0 pad_maximum_fusion.2
  112.3 43.1 %all-gather.4.cloned.1.call-done = bf16[640,4096]{1,0:T(8,128)(2,1)} async-done(((bf16[40,4096]{1,0:T(8,128)(2,1)}), bf16[640,4096]{1,0:T(8,128)(2,1)}) %all-gather.4.cloned.1.call-update) | async-done | bytes 5242896 | tf_op jit(solution)/shard_map/all_gather | solution.py:99
  155.4 1.7 slice.135
  157.1 94.1 %all-gather.6.cloned.1.call-done = bf16[48,28,4096]{2,1,0:T(8,128)(2,1)} async-done(((bf16[3,28,4096]{2,1,0:T(8,128)(2,1)}), bf16[48,28,4096]{2,1,0:T(8,128)(2,1)}) %all-gather.6.cloned.1.call-update) | async-done | bytes 11010064 | tf_op jit(solution)/shard_map/all_gather | solution.py:68
  251.2 5.8 %convolution_bitcast_fusion.2 = f32[2,256,16,28]{1,3,0,2:T(8,128)S(1)} fusion(bf16[16,3,28,4096]{3,2,1,0:T(8,128)(2,1)} %bitcast.244, bf16[256,4096,1,1]{1,0,3,2:T(8,128)(2,1)S(1)} %bitcast.222), kind=kOutput, calls=%fused_computation.51 | convolution fusion | flops 1879048192 | bytes 14024704 | tf_op jit(solution)/shard_map/rd,jkud->krju/dot_general | solution.py:107
  256.9 4.9 %fusion.12 = bf16[256,4096]{1,0:T(8,128)(2,1)} fusion(bf16[16,3,28,4096]{3,2,1,0:T(8,128)(2,1)} %bitcast.245, f32[2,256,16,28]{1,3,0,2:T(8,128)S(1)} %convolution_bitcast_fusion.2), kind=kOutput, calls=%fused_computation.25 | convolution fusion | flops 941260800 | bytes 7208960 | tf_op jit(solution)/shard_map/rju,jud->rd/dot_general | solution.py:111
  261.9 2.2 slice.131
  264.1 7.2 %convolution_bitcast_fusion.1 = f32[2,384,16,28]{1,3,0,2:T(8,128)S(1)} fusion(bf16[16,3,28,4096]{3,2,1,0:T(8,128)(2,1)} %bitcast.246, bf16[384,4096,1,1]{1,0,3,2:T(8,128)(2,1)S(1)} %bitcast.221), kind=kOutput, calls=%fused_computation.50 | convolution fusion | flops 2818572288 | bytes 15532032 | tf_op jit(solution)/shard_map/rd,jkud->krju/dot_general | solution.py:107
  271.4 5.8 %bitcast_convert_fusion = bf16[384,4096]{1,0:T(8,128)(2,1)} fusion(bf16[16,3,28,4096]{3,2,1,0:T(8,128)(2,1)} %bitcast.247, f32[2,384,16,28]{1,3,0,2:T(8,128)S(1)} %convolution_bitcast_fusion.1), kind=kOutput, calls=%fused_computation.23 | convolution fusion | flops 1411891200 | bytes 8716288 | tf_op jit(solution)/shard_map/rju,jud->rd/dot_general | solution.py:111
  277.3 1.5 convert_element_type.146
  278.8 1.9 copy.96
  280.8 41.0 %reduce-scatter.5.cloned.1.call-done = bf16[16,4096]{1,0:T(8,128)(2,1)} async-done(((bf16[256,4096]{1,0:T(8,128)(2,1)}), bf16[16,4096]{1,0:T(8,128)(2,1)}) %reduce-scatter.5.cloned.1.call-update) | async-done | bytes 131088 | tf_op jit(solution)/shard_map/reduce_scatter | solution.py:115
  321.7 62.6 %reduce-scatter.3.cloned.1.call-done = bf16[24,4096]{1,0:T(8,128)(2,1)} async-done(((bf16[384,4096]{1,0:T(8,128)(2,1)}), bf16[24,4096]{1,0:T(8,128)(2,1)}) %reduce-scatter.3.cloned.1.call-update) | async-done | bytes 196624 | tf_op jit(solution)/shard_map/reduce_scatter | solution.py:115
  384.3 1.0 maximum_convert_fusion
  385.3 2.6 gather_fusion.2
  387.9 3.1 fusion.30
  (64 shorter events, 2.5 us)
Async XLA Ops:
  6.5 14.9 %copy-start.14 = (s32[1,16]{1,0:T(1,128)S(1)}, s32[1,16]{1,0:T(1,128)}, u32[]{:S(2)}) copy-start(s32[1,16]{1,0:T(1,128)} %param.12) | copy-start | bytes 196
  14.0 34.6 %all-to-all-start = ((bf16[16,128,512]{2,1,0:T(8,128)(2,1)}), bf16[16,128,512]{2,1,0:T(8,128)(2,1)S(1)}, u32[]{:S(2)}, u32[]{:S(2)}) async-start(bf16[16,128,512]{2,1,0:T(8,128)(2,1)} %pad_maximum_fusion), calls=%async_computation | async-start | bytes 4194304 | tf_op jit(solution)/shard_map/all_to_all | solution.py:76
  53.0 3.8 copy-start.2
  53.3 8.9 %copy-start.5 = (bf16[16,128,128]{2,1,0:T(8,128)(2,1)}, bf16[16,128,128]{2,1,0:T(8,128)(2,1)S(1)}, u32[]{:S(2)}) copy-start(bf16[16,128,128]{2,1,0:T(8,128)(2,1)S(1)} %get-tuple-element.11) | copy-start | bytes 1572868
  53.3 13.3 %copy-start.3 = (bf16[16,128,128]{2,1,0:T(8,128)(2,1)}, bf16[16,128,128]{2,1,0:T(8,128)(2,1)S(1)}, u32[]{:S(2)}) copy-start(bf16[16,128,128]{2,1,0:T(8,128)(2,1)S(1)} %get-tuple-element.12) | copy-start | bytes 1572868
  58.9 3.3 copy-start.1
  58.9 3.3 copy-start.8
  66.6 4.4 %copy-start = (pred[512,2048]{0,1:T(8,128)(4,1)S(1)}, pred[512,2048]{0,1:T(8,128)(4,1)}, u32[]{:S(2)}) copy-start(pred[512,2048]{0,1:T(8,128)(4,1)} %get-tuple-element.14) | copy-start | bytes 3145732
  71.0 5.0 %copy-start.4 = (bf16[16,128,128]{2,1,0:T(8,128)(2,1)S(1)}, bf16[16,128,128]{2,1,0:T(8,128)(2,1)}, u32[]{:S(2)}) copy-start(bf16[16,128,128]{2,1,0:T(8,128)(2,1)} %copy-done.3) | copy-start | bytes 1572868
  75.9 3.4 copy-start.6
  83.8 2.7 copy-start.10
  83.8 2.7 copy-start.11
  83.8 2.7 copy-start.12
  83.8 11.0 %copy-start.15 = (s32[1,128,2]{1,2,0:T(2,128)S(1)}, s32[1,128,2]{1,2,0:T(2,128)}, u32[]{:S(2)}) copy-start(s32[1,128,2]{1,2,0:T(2,128)} %param.13) | copy-start | bytes 3076
  86.5 22.5 %copy-start.13 = (f32[4096]{0:T(1024)S(1)}, f32[4096]{0:T(1024)}, u32[]{:S(2)}) copy-start(f32[4096]{0:T(1024)} %param.15) | copy-start | bytes 49156
  86.5 24.5 %copy-start.7 = (bf16[2,28,4096]{2,0,1:T(2,128)(2,1)S(1)}, bf16[2,28,4096]{2,0,1:T(2,128)(2,1)}, u32[]{:S(2)}) copy-start(bf16[2,28,4096]{2,0,1:T(2,128)(2,1)} %param.16) | copy-start | bytes 1376260
  86.5 24.8 %copy-start.9 = (bf16[28,4096]{1,0:T(8,128)(2,1)S(1)}, bf16[28,4096]{1,0:T(8,128)(2,1)}, u32[]{:S(2)}) copy-start(bf16[28,4096]{1,0:T(8,128)(2,1)} %param.17) | copy-start | bytes 688132
  88.0 19.8 %all-to-all-start.1 = ((bf16[16,128,256]{2,1,0:T(8,128)(2,1)}), bf16[16,128,256]{2,1,0:T(8,128)(2,1)S(1)}, u32[]{:S(2)}, u32[]{:S(2)}) async-start(bf16[16,128,256]{2,1,0:T(8,128)(2,1)} %bitcast.43), calls=%async_computation.1 | async-start | bytes 2097152 | tf_op jit(solution)/shard_map/all_to_all | solution.py:84
  94.8 60.5 %all-gather.4.cloned.1.call-start = ((), (), s32[]{:S(2)}) async-start(), calls=%async_computation.4 | async-start | bytes 5570560 | tf_op jit(solution)/shard_map/all_gather | solution.py:99
  110.9 140.3 %all-gather.6.cloned.1.call-start = ((), (), s32[]{:S(2)}) async-start(), calls=%async_computation.7 | async-start | bytes 13369344 | tf_op jit(solution)/shard_map/all_gather | solution.py:68
  112.2 209.5 %reduce-scatter.5.cloned.1.call-start = ((), (), s32[]{:S(2)}) async-start(), calls=%async_computation.6 | async-start | bytes 2228224 | tf_op jit(solution)/shard_map/reduce_scatter | solution.py:115
  261.8 122.4 %reduce-scatter.3.cloned.1.call-start = ((), (), s32[]{:S(2)}) async-start(), calls=%async_computation.5 | async-start | bytes 3342336 | tf_op jit(solution)/shard_map/reduce_scatter | solution.py:115
  271.4 5.9 %copy-start.16 = (f32[1,128,2]{1,2,0:T(2,128)S(1)}, f32[1,128,2]{1,2,0:T(2,128)}, u32[]{:S(2)}) copy-start(f32[1,128,2]{1,2,0:T(2,128)} %param.14) | copy-start | bytes 3076
Sparse Core Ops, SparseCore 0:
  111.0 44.2 all-gather.3
  157.8 93.2 all-gather.5
  262.0 59.7 reduce-scatter.4
  324.1 60.1 reduce-scatter.2

commit v5 on v1

--- a/solution.py
+++ b/solution.py
@@ -64,8 +64,9 @@
     feat = per_dev * HD
     kv_of_dest = (jnp.arange(seq_count) * per_dev) // (QH // KVH)
 
-    weights_local = jnp.concatenate([w_in, w_down[None]], axis=0)[None]
-    weights_all = lax.all_gather(weights_local, "seq", axis=0, tiled=True)
+    weights_local = jnp.concatenate([w_in, w_down[None]], axis=0).reshape(-1)
+    weights_flat = lax.all_gather(weights_local, "seq", axis=0, tiled=True)
+    weights_all = weights_flat.reshape((seq_count,) + (3,) + w_down.shape)
 
     query_send = jnp.transpose(query_rows[0].reshape(tok_count, seq_count, feat), (1, 0, 2))
     key_send = jnp.transpose(key_rows[0].reshape(tok_count, KVH, HD)[:, kv_of_dest, :], (1, 0, 2))

time: 348 us -> 278 us (0.80)
  waiting for transfers between devices: 236 us -> 146 us
  local copies, waits for them, and re-layouts: 18.4 us -> 38.8 us
    all_gather x1, waiting for transfers between devices: 95.8 us -> 0.02 us  [shards_body(): weights_flat = lax.all_gather(weights_local, 'seq', axis=0, tiled=True)]
    reshape x0 -> x2, local copies, waits for them, and re-layouts: none -> 17.6 us  [the longest x1 16.3 us: shards_body(): weights_all = weights_flat.reshape((seq_count,) + (3,) + w_down.shape)]
    all_gather x1, waiting for transfers between devices: 43.1 us -> 27 us  [shards_body(): gathered = lax.all_gather(dispatched, 'grp', axis=0, tiled=True)]
    all_to_all x1, waiting for transfers between devices: 12.4 us -> 25.1 us  [shards_body(): lax.all_to_all(attended.reshape(seq_count, tok_count, feat), 'seq', 0, 0,...]
    all_to_all x1, waiting for transfers between devices: 23.2 us -> 33.7 us  [shards_body(): packed_all = lax.all_to_all(packed, 'seq', 0, 0, tiled=False)]
  transfers between devices with their start and end apart: 5 -> 5, of which waited for: 5 -> 4; matrix products, arithmetic and copies ran while one was open for 3% -> 27% of each run, Pallas kernels for 0% -> 0%
where the time goes in v5:
time: 278 us; the launch traced here: 277 us
  waiting for transfers between devices  146 us (53%)
  matrix products  42.1 us (15%)
  local copies, waits for them, and re-layouts  38.8 us (14%)
  other arithmetic  22.9 us (8%)
  between operations  13.5 us (5%)
  starting transfers between devices  13.2 us (5%)
    reduce_scatter x1, waiting for transfers between devices, shards_body(): lax.psum_scatter(terms.astype(jnp.bfloat16), 'grp', scatter_dimension=0,...  60.4 us
    all_to_all x1, waiting for transfers between devices, shards_body(): packed_all = lax.all_to_all(packed, 'seq', 0, 0, tiled=False)  33.7 us
    all_gather x1, waiting for transfers between devices, shards_body(): gathered = lax.all_gather(dispatched, 'grp', axis=0, tiled=True)  27 us
    all_to_all x1, waiting for transfers between devices, shards_body(): lax.all_to_all(attended.reshape(seq_count, tok_count, feat), 'seq', 0, 0,...  25.1 us
    reshape x1, local copies, waits for them, and re-layouts, shards_body(): weights_all = weights_flat.reshape((seq_count,) + (3,) + w_down.shape)  16.3 us
    dot_general x4, matrix products, attend(): jnp.einsum('gqt,td->qgd', weights.astype(jnp.bfloat16), value_all, prefer...  12.9 us
    dot_general x1, matrix products, shards_body(): jnp.einsum('rd,jkud->krju', gathered, weights_all[:, :2], preferred_eleme...  10.7 us
    dot_general x4, matrix products, attend(): jnp.einsum('qgd,td->gqt', query_tile, key_all, preferred_element_type=jnp...  9.81 us
  transfers between devices with their start and end apart: 5, of which 4 were waited for; matrix products, arithmetic and copies ran while one was open for 27% of the time, Pallas kernels for 0%

profile of v5, /device:TPU:2, one launch (start us, length us, event | category | flops | bytes accessed | tf_op | source)
XLA Modules:
  0.0 276.9 jit_solution(5895107064908455876)
XLA Ops:
  6.5 1.5 copy.91
  8.1 2.0 pad_maximum_fusion.2
  10.0 0.5 copy.92
  10.5 1.3 reshape.255
  11.8 1.1 copy.76
  13.2 1.1 copy.74
  14.5 0.6 gather_fusion.1
  15.2 0.6 gather_fusion
  16.1 0.3 copy.120
  16.4 1.6 pad_maximum_fusion
  18.1 7.5 %all-to-all-start = ((bf16[16,128,512]{2,1,0:T(8,128)(2,1)}), bf16[16,128,512]{2,1,0:T(8,128)(2,1)S(1)}, u32[]{:S(2)}, u32[]{:S(2)}) async-start(bf16[16,128,512]{2,1,0:T(8,128)(2,1)} %pad_maximum_fusion), calls=%async_computation | async-start | bytes 4194304 | tf_op jit(solution)/shard_map/all_to_all | solution.py:77
  25.8 3.6 %broadcast_compare_fusion.3 = (pred[512,2048]{0,1:T(8,128)(4,1)S(1)}, pred[512,2048]{0,1:T(8,128)(4,1)}, pred[512,2048]{0,1:T(8,128)(4,1)}, pred[512,2048]{0,1:T(8,128)(4,1)}) fusion(s32[512]{0:T(512)S(1)} %get-tuple-element.32, s32[2048]{0:T(1024)S(1)} %broadcast_bitcast_fusion, s32[512]{0:T(512)S(1)} %get-tuple-element.31, s32[512]{0:T(512)S(1)} %get-tuple-element.30, ...), kind=kLoop, calls=%fused_computation.49 | loop fusion | flops 4194304 | bytes 4210688 | tf_op jit(solution)/shard_map/eq | solution.py:30
  29.5 33.7 %all-to-all-done = bf16[16,128,512]{2,1,0:T(8,128)(2,1)S(1)} async-done(((bf16[16,128,512]{2,1,0:T(8,128)(2,1)}), bf16[16,128,512]{2,1,0:T(8,128)(2,1)S(1)}, u32[]{:S(2)}, u32[]{:S(2)}) %all-to-all-start) | async-done | bytes 2097184 | tf_op jit(solution)/shard_map/all_to_all | solution.py:77
  63.1 0.9 fusion.98
  64.1 1.7 slice.96
  65.8 1.7 slice.92
  67.5 1.7 slice.88
  69.2 0.8 slice.84
  70.0 1.0 fusion.99
  71.0 3.1 %fusion.11 = (f32[2,512]{1,0:T(2,128)S(1)}, f32[2048,512,2]{1,0,2:T(8,128)S(1)}) fusion(pred[512,2048]{0,1:T(8,128)(4,1)} %get-tuple-element.16, bf16[2048,128,1]{1,0,2:T(8,128)(2,1)S(1)} %bitcast.210, bf16[512,2,128]{2,1,0:T(2,128)(2,1)} %slice.96), kind=kOutput, calls=%fused_computation.23 | convolution fusion | flops 543161344 | bytes 10227712 | tf_op jit(solution)/shard_map/qgd,td->gqt/dot_general | solution.py:32
  74.2 2.2 fusion.10
  76.5 2.2 fusion.9
  78.7 2.2 fusion.8
  80.9 2.0 fusion.6
  82.9 2.0 fusion.4
  85.0 2.0 fusion.2
  87.0 2.2 fusion
  89.2 3.8 %fusion.51 = bf16[512,2,128]{0,2,1:T(8,128)(2,1)S(1)} fusion(bf16[2048,128,1]{1,0,2:T(8,128)(2,1)S(1)} %bitcast.206, f32[2048,512,2]{1,0,2:T(8,128)S(1)} %get-tuple-element.22, f32[2,512]{1,0:T(2,128)S(1)} %get-tuple-element.21, pred[512,2048]{0,1:T(8,128)(4,1)} %get-tuple-element.16, f32[512,2]{0,1:T(2,128)S(1)} %bitcast.223), kind=kOutput, calls=%fused_computation.60 | convolution fusion | flops 545521664 | bytes 10231808 | tf_op jit(solution)/shard_map/gqt,td->qgd/dot_general | solution.py:39
  93.1 3.8 %fusion.57 = bf16[512,2,128]{0,2,1:T(8,128)(2,1)S(1)} fusion(bf16[2048,128,1]{1,0,2:T(8,128)(2,1)S(1)} %bitcast.207, f32[2048,512,2]{1,0,2:T(8,128)S(1)} %get-tuple-element.24, f32[2,512]{1,0:T(2,128)S(1)} %get-tuple-element.23, pred[512,2048]{0,1:T(8,128)(4,1)} %get-tuple-element.15, f32[512,2]{0,1:T(2,128)S(1)} %bitcast.222), kind=kOutput, calls=%fused_computation.62 | convolution fusion | flops 545521664 | bytes 10231808 | tf_op jit(solution)/shard_map/gqt,td->qgd/dot_general | solution.py:39
  96.9 2.6 fusion.63
  99.6 2.6 fusion.69
  102.3 1.3 copy.87
  103.6 5.6 %all-to-all-start.1 = ((bf16[16,128,256]{2,1,0:T(8,128)(2,1)}), bf16[16,128,256]{2,1,0:T(8,128)(2,1)S(1)}, u32[]{:S(2)}, u32[]{:S(2)}) async-start(bf16[16,128,256]{2,1,0:T(8,128)(2,1)} %bitcast.43), calls=%async_computation.1 | async-start | bytes 2097152 | tf_op jit(solution)/shard_map/all_to_all | solution.py:85
  109.7 25.1 %all-to-all-done.1 = bf16[16,128,256]{2,1,0:T(8,128)(2,1)S(1)} async-done(((bf16[16,128,256]{2,1,0:T(8,128)(2,1)}), bf16[16,128,256]{2,1,0:T(8,128)(2,1)S(1)}, u32[]{:S(2)}, u32[]{:S(2)}) %all-to-all-start.1) | async-done | bytes 1048608 | tf_op jit(solution)/shard_map/all_to_all | solution.py:85
  134.9 0.7 copy.88
  135.6 0.6 multiply_reduce_fusion
  136.1 0.7 fusion.27
  136.8 1.2 convolution_convert_fusion
  138.1 16.3 %reshape.256 = bf16[16,3,28,4096]{3,2,1,0:T(8,128)(2,1)} reshape(bf16[5505024]{0:T(1024)(128)(2,1)} %all-gather.3.cloned.1.call-done) | data formatting | bytes 22020096 | tf_op jit(solution)/shard_map/reshape | solution.py:69
  154.4 27.0 %all-gather.5.cloned.1.call-done = bf16[640,4096]{1,0:T(8,128)(2,1)} async-done(((bf16[40,4096]{1,0:T(8,128)(2,1)}), bf16[640,4096]{1,0:T(8,128)(2,1)}) %all-gather.5.cloned.1.call-update) | async-done | bytes 5242896 | tf_op jit(solution)/shard_map/all_gather | solution.py:100
  181.5 10.7 %fusion.32 = f32[2,640,16,28]{1,3,0,2:T(8,128)S(1)} fusion(bf16[16,3,28,4096]{3,2,1,0:T(8,128)(2,1)} %reshape.256, bf16[640,4096]{1,0:T(8,128)(2,1)} %all-gather.5.cloned.1.call-done), kind=kOutput, calls=%fused_computation.50 | convolution fusion | flops 4697620480 | bytes 18546688 | tf_op jit(solution)/shard_map/rd,jkud->krju/dot_general | solution.py:101
  192.2 7.5 %bitcast_convert_fusion = bf16[640,4096]{1,0:T(8,128)(2,1)} fusion(bf16[16,3,28,4096]{3,2,1,0:T(8,128)(2,1)} %reshape.256, f32[2,640,16,28]{1,3,0,2:T(8,128)S(1)} %fusion.32), kind=kOutput, calls=%fused_computation.3 | convolution fusion | flops 2353152000 | bytes 11730944 | tf_op jit(solution)/shard_map/rju,jud->rd/dot_general | solution.py:105
  199.8 1.6 convert_element_type.134
  201.4 1.9 copy.100
  203.3 60.4 %reduce-scatter.2.cloned.1.call-done = bf16[40,4096]{1,0:T(8,128)(2,1)} async-done(((bf16[640,4096]{1,0:T(8,128)(2,1)}), bf16[40,4096]{1,0:T(8,128)(2,1)}) %reduce-scatter.2.cloned.1.call-update) | async-done | bytes 327696 | tf_op jit(solution)/shard_map/reduce_scatter | solution.py:108
  263.7 1.0 convert_element_type.129
  264.7 2.6 gather_fusion.2
  267.3 3.1 %fusion.31 = bf16[1,128,4096]{2,1,0:T(8,128)(2,1)} fusion(f32[1,128,4096]{2,1,0:T(8,128)S(1)} %copy.100, f32[128,4096]{1,0:T(8,128)} %gather_fusion.2, f32[128]{0:T(128)S(1)} %select_reduce_fusion, pred[128]{0:T(512)(128)(4,1)S(1)} %compare_and_fusion, pred[128]{0:T(512)(128)(4,1)S(1)} %fusion.88), kind=kLoop, calls=%fused_computation.44 | loop fusion | flops 2621440 | bytes 5243648 | tf_op jit(solution)/shard_map/convert_element_type | solution.py:114
  (50 shorter events, 1.7 us)
Async XLA Ops:
  6.5 9.3 %copy-start.3 = (bf16[1,128,4096]{2,1,0:T(8,128)(2,1)S(1)}, bf16[1,128,4096]{2,1,0:T(8,128)(2,1)}, u32[]{:S(2)}) copy-start(bf16[1,128,4096]{2,1,0:T(8,128)(2,1)} %param.9) | copy-start | bytes 3145732
  6.5 131.6 %all-gather.3.cloned.1.call-start = ((), (), s32[]{:S(2)}) async-start(), calls=%async_computation.3 | async-start | bytes 11698176 | tf_op jit(solution)/shard_map/all_gather | solution.py:68
  11.8 13.7 %copy-start.9 = (s32[1,16]{1,0:T(1,128)S(1)}, s32[1,16]{1,0:T(1,128)}, u32[]{:S(2)}) copy-start(s32[1,16]{1,0:T(1,128)} %param.12) | copy-start | bytes 196
  18.1 45.1 %all-to-all-start = ((bf16[16,128,512]{2,1,0:T(8,128)(2,1)}), bf16[16,128,512]{2,1,0:T(8,128)(2,1)S(1)}, u32[]{:S(2)}, u32[]{:S(2)}) async-start(bf16[16,128,512]{2,1,0:T(8,128)(2,1)} %pad_maximum_fusion), calls=%async_computation | async-start | bytes 4194304 | tf_op jit(solution)/shard_map/all_to_all | solution.py:77
  70.0 4.1 %copy-start.1 = (pred[512,2048]{0,1:T(8,128)(4,1)S(1)}, pred[512,2048]{0,1:T(8,128)(4,1)}, u32[]{:S(2)}) copy-start(pred[512,2048]{0,1:T(8,128)(4,1)} %get-tuple-element.15) | copy-start | bytes 3145732
  70.0 4.2 %copy-start.7 = (bf16[512,2,128]{2,1,0:T(2,128)(2,1)S(1)}, bf16[512,2,128]{2,1,0:T(2,128)(2,1)}, u32[]{:S(2)}) copy-start(bf16[512,2,128]{2,1,0:T(2,128)(2,1)} %slice.92) | copy-start | bytes 786436
  74.2 2.3 copy-start
  74.2 2.3 copy-start.6
  76.4 2.3 copy-start.5
  78.7 2.2 copy-start.2
  85.0 4.3 %copy-start.4 = (bf16[16,128,128]{2,1,0:T(8,128)(2,1)S(1)}, bf16[16,128,128]{2,1,0:T(8,128)(2,1)}, u32[]{:S(2)}) copy-start(bf16[16,128,128]{2,1,0:T(8,128)(2,1)} %get-tuple-element.12) | copy-start | bytes 1572868
  99.5 9.8 %copy-start.10 = (s32[1,128,2]{1,2,0:T(2,128)S(1)}, s32[1,128,2]{1,2,0:T(2,128)}, u32[]{:S(2)}) copy-start(s32[1,128,2]{1,2,0:T(2,128)} %param.13) | copy-start | bytes 3076
  102.2 33.9 %copy-start.8 = (f32[4096]{0:T(1024)S(1)}, f32[4096]{0:T(1024)}, u32[]{:S(2)}) copy-start(f32[4096]{0:T(1024)} %param.15) | copy-start | bytes 49156
  103.6 31.3 %all-to-all-start.1 = ((bf16[16,128,256]{2,1,0:T(8,128)(2,1)}), bf16[16,128,256]{2,1,0:T(8,128)(2,1)S(1)}, u32[]{:S(2)}, u32[]{:S(2)}) async-start(bf16[16,128,256]{2,1,0:T(8,128)(2,1)} %bitcast.43), calls=%async_computation.1 | async-start | bytes 2097152 | tf_op jit(solution)/shard_map/all_to_all | solution.py:85
  109.2 72.2 %all-gather.5.cloned.1.call-start = ((), (), s32[]{:S(2)}) async-start(), calls=%async_computation.4 | async-start | bytes 5570560 | tf_op jit(solution)/shard_map/all_gather | solution.py:100
  138.0 125.7 %reduce-scatter.2.cloned.1.call-start = ((), (), s32[]{:S(2)}) async-start(), calls=%async_computation.5 | async-start | bytes 5570560 | tf_op jit(solution)/shard_map/reduce_scatter | solution.py:108
  192.2 7.6 %copy-start.11 = (f32[1,128,2]{1,2,0:T(2,128)S(1)}, f32[1,128,2]{1,2,0:T(2,128)}, u32[]{:S(2)}) copy-start(f32[1,128,2]{1,2,0:T(2,128)} %param.14) | copy-start | bytes 3076
Sparse Core Ops, SparseCore 0:
  12.0 122.6 all-gather.2
  138.2 43.2 all-gather.4
  199.9 63.8 reduce-scatter.1

commit v6 on v5

--- a/solution.py
+++ b/solution.py
@@ -62,16 +62,18 @@
     tok_count = query_rows.shape[1]
     per_dev = QH // seq_count
     feat = per_dev * HD
-    kv_of_dest = (jnp.arange(seq_count) * per_dev) // (QH // KVH)
 
     weights_local = jnp.concatenate([w_in, w_down[None]], axis=0).reshape(-1)
     weights_flat = lax.all_gather(weights_local, "seq", axis=0, tiled=True)
     weights_all = weights_flat.reshape((seq_count,) + (3,) + w_down.shape)
 
     query_send = jnp.transpose(query_rows[0].reshape(tok_count, seq_count, feat), (1, 0, 2))
-    key_send = jnp.transpose(key_rows[0].reshape(tok_count, KVH, HD)[:, kv_of_dest, :], (1, 0, 2))
-    value_send = jnp.transpose(
-        value_rows[0].reshape(tok_count, KVH, HD)[:, kv_of_dest, :], (1, 0, 2)
+    kv_repeat = seq_count // KVH
+    key_send = jnp.repeat(
+        jnp.transpose(key_rows[0].reshape(tok_count, KVH, HD), (1, 0, 2)), kv_repeat, axis=0
+    )
+    value_send = jnp.repeat(
+        jnp.transpose(value_rows[0].reshape(tok_count, KVH, HD), (1, 0, 2)), kv_repeat, axis=0
     )
     packed = jnp.concatenate([query_send, key_send, value_send], axis=2)
     packed_all = lax.all_to_all(packed, "seq", 0, 0, tiled=False)

time: 278 us -> 276 us (level)
  transfers between devices with their start and end apart: 5 -> 5, of which waited for: 4 -> 4; matrix products, arithmetic and copies ran while one was open for 27% -> 26% of each run, Pallas kernels for 0% -> 0%
where the time goes in v6:
time: 276 us; the launch traced here: 275 us
  waiting for transfers between devices  146 us (53%)
  matrix products  42.1 us (15%)
  local copies, waits for them, and re-layouts  37.2 us (13%)
  other arithmetic  22.8 us (8%)
  between operations  13.5 us (5%)
  starting transfers between devices  13.2 us (5%)
    reduce_scatter x1, waiting for transfers between devices, shards_body(): lax.psum_scatter(terms.astype(jnp.bfloat16), 'grp', scatter_dimension=0,...  60.2 us
    all_to_all x1, waiting for transfers between devices, shards_body(): packed_all = lax.all_to_all(packed, 'seq', 0, 0, tiled=False)  33.4 us
    all_gather x1, waiting for transfers between devices, shards_body(): gathered = lax.all_gather(dispatched, 'grp', axis=0, tiled=True)  27.1 us
    all_to_all x1, waiting for transfers between devices, shards_body(): lax.all_to_all(attended.reshape(seq_count, tok_count, feat), 'seq', 0, 0,...  25.2 us
    reshape x1, local copies, waits for them, and re-layouts, shards_body(): weights_all = weights_flat.reshape((seq_count,) + (3,) + w_down.shape)  16.3 us
    dot_general x4, matrix products, attend(): jnp.einsum('gqt,td->qgd', weights.astype(jnp.bfloat16), value_all, prefer...  12.9 us
    dot_general x1, matrix products, shards_body(): jnp.einsum('rd,jkud->krju', gathered, weights_all[:, :2], preferred_eleme...  10.7 us
    dot_general x4, matrix products, attend(): jnp.einsum('qgd,td->gqt', query_tile, key_all, preferred_element_type=jnp...  9.81 us
  transfers between devices with their start and end apart: 5, of which 4 were waited for; matrix products, arithmetic and copies ran while one was open for 26% of the time, Pallas kernels for 0%

profile of v6, /device:TPU:2, one launch (start us, length us, event | category | flops | bytes accessed | tf_op | source)
XLA Modules:
  0.0 274.7 jit_solution(366741255312686342)
XLA Ops:
  6.5 1.5 copy.72
  8.1 2.0 pad_maximum_fusion.2
  10.0 0.5 copy.73
  10.5 1.3 reshape.202
  11.8 1.0 copy.85
  12.9 1.0 copy.84
  13.9 0.2 copy.83
  14.2 0.3 copy.103
  14.7 1.6 pad_maximum_fusion
  16.3 7.5 %all-to-all-start = ((bf16[16,128,512]{2,1,0:T(8,128)(2,1)}), bf16[16,128,512]{2,1,0:T(8,128)(2,1)S(1)}, u32[]{:S(2)}, u32[]{:S(2)}) async-start(bf16[16,128,512]{2,1,0:T(8,128)(2,1)} %pad_maximum_fusion), calls=%async_computation | async-start | bytes 4194304 | tf_op jit(solution)/shard_map/all_to_all | solution.py:79
  24.1 3.7 %broadcast_compare_fusion.3 = (pred[512,2048]{0,1:T(8,128)(4,1)S(1)}, pred[512,2048]{0,1:T(8,128)(4,1)}, pred[512,2048]{0,1:T(8,128)(4,1)}, pred[512,2048]{0,1:T(8,128)(4,1)}) fusion(s32[512]{0:T(512)S(1)} %get-tuple-element.32, s32[2048]{0:T(1024)S(1)} %broadcast_bitcast_fusion, s32[512]{0:T(512)S(1)} %get-tuple-element.31, s32[512]{0:T(512)S(1)} %get-tuple-element.30, ...), kind=kLoop, calls=%fused_computation.47 | loop fusion | flops 4194304 | bytes 4210688 | tf_op jit(solution)/shard_map/eq | solution.py:30
  27.8 33.4 %all-to-all-done = bf16[16,128,512]{2,1,0:T(8,128)(2,1)S(1)} async-done(((bf16[16,128,512]{2,1,0:T(8,128)(2,1)}), bf16[16,128,512]{2,1,0:T(8,128)(2,1)S(1)}, u32[]{:S(2)}, u32[]{:S(2)}) %all-to-all-start) | async-done | bytes 2097184 | tf_op jit(solution)/shard_map/all_to_all | solution.py:79
  61.2 0.9 fusion.97
  62.1 1.7 slice.96
  63.8 1.7 slice.92
  65.6 1.7 slice.88
  67.3 0.8 slice.84
  68.1 1.0 fusion.98
  69.0 3.1 %fusion.11 = (f32[2,512]{1,0:T(2,128)S(1)}, f32[2048,512,2]{1,0,2:T(8,128)S(1)}) fusion(pred[512,2048]{0,1:T(8,128)(4,1)} %get-tuple-element.16, bf16[2048,128,1]{1,0,2:T(8,128)(2,1)S(1)} %bitcast.220, bf16[512,2,128]{2,1,0:T(2,128)(2,1)} %slice.96), kind=kOutput, calls=%fused_computation.21 | convolution fusion | flops 543161344 | bytes 10227712 | tf_op jit(solution)/shard_map/qgd,td->gqt/dot_general | solution.py:32
  72.2 2.2 fusion.10
  74.5 2.2 fusion.9
  76.7 2.2 fusion.8
  79.0 2.0 fusion.6
  81.0 2.0 fusion.4
  83.0 2.0 fusion.2
  85.0 2.2 fusion
  87.3 3.8 %fusion.51 = bf16[512,2,128]{0,2,1:T(8,128)(2,1)S(1)} fusion(bf16[2048,128,1]{1,0,2:T(8,128)(2,1)S(1)} %bitcast.216, f32[2048,512,2]{1,0,2:T(8,128)S(1)} %get-tuple-element.22, f32[2,512]{1,0:T(2,128)S(1)} %get-tuple-element.21, pred[512,2048]{0,1:T(8,128)(4,1)} %get-tuple-element.16, f32[512,2]{0,1:T(2,128)S(1)} %bitcast.235), kind=kOutput, calls=%fused_computation.58 | convolution fusion | flops 545521664 | bytes 10231808 | tf_op jit(solution)/shard_map/gqt,td->qgd/dot_general | solution.py:39
  91.1 3.8 %fusion.57 = bf16[512,2,128]{0,2,1:T(8,128)(2,1)S(1)} fusion(bf16[2048,128,1]{1,0,2:T(8,128)(2,1)S(1)} %bitcast.217, f32[2048,512,2]{1,0,2:T(8,128)S(1)} %get-tuple-element.24, f32[2,512]{1,0:T(2,128)S(1)} %get-tuple-element.23, pred[512,2048]{0,1:T(8,128)(4,1)} %get-tuple-element.15, f32[512,2]{0,1:T(2,128)S(1)} %bitcast.234), kind=kOutput, calls=%fused_computation.60 | convolution fusion | flops 545521664 | bytes 10231808 | tf_op jit(solution)/shard_map/gqt,td->qgd/dot_general | solution.py:39
  95.0 2.6 fusion.63
  97.6 2.6 fusion.69
  100.4 1.3 copy.68
  101.7 5.6 %all-to-all-start.1 = ((bf16[16,128,256]{2,1,0:T(8,128)(2,1)}), bf16[16,128,256]{2,1,0:T(8,128)(2,1)S(1)}, u32[]{:S(2)}, u32[]{:S(2)}) async-start(bf16[16,128,256]{2,1,0:T(8,128)(2,1)} %bitcast.44), calls=%async_computation.1 | async-start | bytes 2097152 | tf_op jit(solution)/shard_map/all_to_all | solution.py:87
  107.5 0.2 reduce-window.4
  107.8 25.2 %all-to-all-done.1 = bf16[16,128,256]{2,1,0:T(8,128)(2,1)S(1)} async-done(((bf16[16,128,256]{2,1,0:T(8,128)(2,1)}), bf16[16,128,256]{2,1,0:T(8,128)(2,1)S(1)}, u32[]{:S(2)}, u32[]{:S(2)}) %all-to-all-start.1) | async-done | bytes 1048608 | tf_op jit(solution)/shard_map/all_to_all | solution.py:87
  133.0 0.7 copy.69
  133.6 0.6 multiply_reduce_fusion
  134.2 0.7 fusion.27
  134.9 1.2 convolution_convert_fusion
  136.2 16.3 %reshape.203 = bf16[16,3,28,4096]{3,2,1,0:T(8,128)(2,1)} reshape(bf16[5505024]{0:T(1024)(128)(2,1)} %all-gather.3.cloned.1.call-done) | data formatting | bytes 22020096 | tf_op jit(solution)/shard_map/reshape | solution.py:68
  152.5 27.1 %all-gather.5.cloned.1.call-done = bf16[640,4096]{1,0:T(8,128)(2,1)} async-done(((bf16[40,4096]{1,0:T(8,128)(2,1)}), bf16[640,4096]{1,0:T(8,128)(2,1)}) %all-gather.5.cloned.1.call-update) | async-done | bytes 5242896 | tf_op jit(solution)/shard_map/all_gather | solution.py:102
  179.5 10.7 %fusion.32 = f32[2,640,16,28]{1,3,0,2:T(8,128)S(1)} fusion(bf16[16,3,28,4096]{3,2,1,0:T(8,128)(2,1)} %reshape.203, bf16[640,4096]{1,0:T(8,128)(2,1)} %all-gather.5.cloned.1.call-done), kind=kOutput, calls=%fused_computation.48 | convolution fusion | flops 4697620480 | bytes 18546688 | tf_op jit(solution)/shard_map/rd,jkud->krju/dot_general | solution.py:103
  190.3 7.5 %bitcast_convert_fusion = bf16[640,4096]{1,0:T(8,128)(2,1)} fusion(bf16[16,3,28,4096]{3,2,1,0:T(8,128)(2,1)} %reshape.203, f32[2,640,16,28]{1,3,0,2:T(8,128)S(1)} %fusion.32), kind=kOutput, calls=%fused_computation.1 | convolution fusion | flops 2353152000 | bytes 11730944 | tf_op jit(solution)/shard_map/rju,jud->rd/dot_general | solution.py:107
  197.9 1.6 convert_element_type.134
  199.4 1.9 copy.81
  201.4 60.2 %reduce-scatter.2.cloned.1.call-done = bf16[40,4096]{1,0:T(8,128)(2,1)} async-done(((bf16[640,4096]{1,0:T(8,128)(2,1)}), bf16[40,4096]{1,0:T(8,128)(2,1)}) %reduce-scatter.2.cloned.1.call-update) | async-done | bytes 327696 | tf_op jit(solution)/shard_map/reduce_scatter | solution.py:110
  261.5 1.0 convert_element_type.129
  262.5 2.6 gather_fusion
  265.1 3.1 %fusion.31 = bf16[1,128,4096]{2,1,0:T(8,128)(2,1)} fusion(f32[1,128,4096]{2,1,0:T(8,128)S(1)} %copy.81, f32[128,4096]{1,0:T(8,128)} %gather_fusion, f32[128]{0:T(128)S(1)} %select_reduce_fusion, pred[128]{0:T(512)(128)(4,1)S(1)} %compare_and_fusion, pred[128]{0:T(512)(128)(4,1)S(1)} %fusion.87), kind=kLoop, calls=%fused_computation.42 | loop fusion | flops 2621440 | bytes 5243648 | tf_op jit(solution)/shard_map/convert_element_type | solution.py:116
  (48 shorter events, 1.2 us)
Async XLA Ops:
  6.5 7.4 %copy-start.3 = (bf16[1,128,4096]{2,1,0:T(8,128)(2,1)S(1)}, bf16[1,128,4096]{2,1,0:T(8,128)(2,1)}, u32[]{:S(2)}) copy-start(bf16[1,128,4096]{2,1,0:T(8,128)(2,1)} %param.9) | copy-start | bytes 3145732
  6.5 129.6 %all-gather.3.cloned.1.call-start = ((), (), s32[]{:S(2)}) async-start(), calls=%async_computation.3 | async-start | bytes 11698176 | tf_op jit(solution)/shard_map/all_gather | solution.py:67
  11.8 12.0 %copy-start.9 = (s32[1,16]{1,0:T(1,128)S(1)}, s32[1,16]{1,0:T(1,128)}, u32[]{:S(2)}) copy-start(s32[1,16]{1,0:T(1,128)} %param.12) | copy-start | bytes 196
  16.3 44.9 %all-to-all-start = ((bf16[16,128,512]{2,1,0:T(8,128)(2,1)}), bf16[16,128,512]{2,1,0:T(8,128)(2,1)S(1)}, u32[]{:S(2)}, u32[]{:S(2)}) async-start(bf16[16,128,512]{2,1,0:T(8,128)(2,1)} %pad_maximum_fusion), calls=%async_computation | async-start | bytes 4194304 | tf_op jit(solution)/shard_map/all_to_all | solution.py:79
  68.1 4.2 %copy-start.1 = (pred[512,2048]{0,1:T(8,128)(4,1)S(1)}, pred[512,2048]{0,1:T(8,128)(4,1)}, u32[]{:S(2)}) copy-start(pred[512,2048]{0,1:T(8,128)(4,1)} %get-tuple-element.15) | copy-start | bytes 3145732
  68.1 4.2 %copy-start.7 = (bf16[512,2,128]{2,1,0:T(2,128)(2,1)S(1)}, bf16[512,2,128]{2,1,0:T(2,128)(2,1)}, u32[]{:S(2)}) copy-start(bf16[512,2,128]{2,1,0:T(2,128)(2,1)} %slice.92) | copy-start | bytes 786436
  72.2 2.3 copy-start
  72.2 2.3 copy-start.6
  74.5 2.3 copy-start.5
  76.7 2.2 copy-start.2
  83.0 4.3 %copy-start.4 = (bf16[16,128,128]{2,1,0:T(8,128)(2,1)S(1)}, bf16[16,128,128]{2,1,0:T(8,128)(2,1)}, u32[]{:S(2)}) copy-start(bf16[16,128,128]{2,1,0:T(8,128)(2,1)} %get-tuple-element.12) | copy-start | bytes 1572868
  97.6 9.7 %copy-start.10 = (s32[1,128,2]{1,2,0:T(2,128)S(1)}, s32[1,128,2]{1,2,0:T(2,128)}, u32[]{:S(2)}) copy-start(s32[1,128,2]{1,2,0:T(2,128)} %param.13) | copy-start | bytes 3076
  100.2 34.0 %copy-start.8 = (f32[4096]{0:T(1024)S(1)}, f32[4096]{0:T(1024)}, u32[]{:S(2)}) copy-start(f32[4096]{0:T(1024)} %param.15) | copy-start | bytes 49156
  101.7 31.3 %all-to-all-start.1 = ((bf16[16,128,256]{2,1,0:T(8,128)(2,1)}), bf16[16,128,256]{2,1,0:T(8,128)(2,1)S(1)}, u32[]{:S(2)}, u32[]{:S(2)}) async-start(bf16[16,128,256]{2,1,0:T(8,128)(2,1)} %bitcast.44), calls=%async_computation.1 | async-start | bytes 2097152 | tf_op jit(solution)/shard_map/all_to_all | solution.py:87
  107.3 72.3 %all-gather.5.cloned.1.call-start = ((), (), s32[]{:S(2)}) async-start(), calls=%async_computation.4 | async-start | bytes 5570560 | tf_op jit(solution)/shard_map/all_gather | solution.py:102
  136.1 125.4 %reduce-scatter.2.cloned.1.call-start = ((), (), s32[]{:S(2)}) async-start(), calls=%async_computation.5 | async-start | bytes 5570560 | tf_op jit(solution)/shard_map/reduce_scatter | solution.py:110
  190.3 7.6 %copy-start.11 = (f32[1,128,2]{1,2,0:T(2,128)S(1)}, f32[1,128,2]{1,2,0:T(2,128)}, u32[]{:S(2)}) copy-start(f32[1,128,2]{1,2,0:T(2,128)} %param.14) | copy-start | bytes 3076
Sparse Core Ops, SparseCore 0:
  12.0 120.8 all-gather.2
  136.2 43.2 all-gather.4
  197.9 63.5 reduce-scatter.1

commit v7 on v6

--- a/solution.py
+++ b/solution.py
@@ -109,9 +109,10 @@
     )
     returned = lax.psum_scatter(
         terms.astype(jnp.bfloat16), "grp", scatter_dimension=0, tiled=True
-    ).astype(jnp.float32)
-    picked_rows = jnp.take(returned, jnp.clip(slot_index, 0, CAP - 1), axis=0)
-    expert_out = jnp.where(routed[:, None], picked_rows, 0.0)
+    )
+    expert_out = jnp.dot(
+        jnp.transpose(onehot).astype(jnp.bfloat16), returned, preferred_element_type=jnp.float32
+    )
     layer_out = attn_float + gate_share[:, None] * expert_out
     return layer_out.astype(jnp.bfloat16)[None]
 

time: 276 us -> 270 us (0.978)
  other arithmetic: 22.8 us -> 16.4 us
  local copies, waits for them, and re-layouts: 37.2 us -> 32.2 us
  waiting for transfers between devices: 146 us -> 150 us
    convert_element_type x4 -> x0, other arithmetic: 6.36 us -> none  [the longest x1 3.07 us: shards_body(): return layer_out.astype(jnp.bfloat16)[None]]
    reduce_scatter x1, waiting for transfers between devices: 60.2 us -> 63.8 us  [shards_body(): lax.psum_scatter(terms.astype(jnp.bfloat16), 'grp', scatter_dimension=0,...]
  transfers between devices with their start and end apart: 5 -> 5, of which waited for: 4 -> 4; matrix products, arithmetic and copies ran while one was open for 26% -> 25% of each run, Pallas kernels for 0% -> 0%
where the time goes in v7:
time: 270 us; the launch traced here: 269 us
  waiting for transfers between devices  150 us (56%)
  matrix products  44.5 us (16%)
  local copies, waits for them, and re-layouts  32.2 us (12%)
  other arithmetic  16.4 us (6%)
  between operations  13.5 us (5%)
  starting transfers between devices  13.2 us (5%)
    reduce_scatter x1, waiting for transfers between devices, shards_body(): lax.psum_scatter(terms.astype(jnp.bfloat16), 'grp', scatter_dimension=0,...  63.8 us
    all_to_all x1, waiting for transfers between devices, shards_body(): packed_all = lax.all_to_all(packed, 'seq', 0, 0, tiled=False)  33.4 us
    all_gather x1, waiting for transfers between devices, shards_body(): gathered = lax.all_gather(dispatched, 'grp', axis=0, tiled=True)  27 us
    all_to_all x1, waiting for transfers between devices, shards_body(): lax.all_to_all(attended.reshape(seq_count, tok_count, feat), 'seq', 0, 0,...  25.2 us
    reshape x1, local copies, waits for them, and re-layouts, shards_body(): weights_all = weights_flat.reshape((seq_count,) + (3,) + w_down.shape)  16.3 us
    dot_general x4, matrix products, attend(): jnp.einsum('gqt,td->qgd', weights.astype(jnp.bfloat16), value_all, prefer...  12.9 us
    dot_general x1, matrix products, shards_body(): jnp.einsum('rd,jkud->krju', gathered, weights_all[:, :2], preferred_eleme...  10.7 us
    dot_general x4, matrix products, attend(): jnp.einsum('qgd,td->gqt', query_tile, key_all, preferred_element_type=jnp...  9.81 us
  transfers between devices with their start and end apart: 5, of which 4 were waited for; matrix products, arithmetic and copies ran while one was open for 25% of the time, Pallas kernels for 0%

profile of v7, /device:TPU:2, one launch (start us, length us, event | category | flops | bytes accessed | tf_op | source)
XLA Modules:
  0.0 269.4 jit_solution(11113787423132224649)
XLA Ops:
  6.5 1.5 copy.52
  8.1 2.0 pad_maximum_fusion.2
  10.0 0.5 copy.53
  10.5 1.3 reshape.111
  11.8 1.0 copy.65
  12.9 1.0 copy.64
  13.9 0.2 copy.63
  14.2 0.3 copy.83
  14.6 0.1 broadcast_in_dim.73
  14.7 1.6 pad_maximum_fusion
  16.3 7.5 %all-to-all-start = ((bf16[16,128,512]{2,1,0:T(8,128)(2,1)}), bf16[16,128,512]{2,1,0:T(8,128)(2,1)S(1)}, u32[]{:S(2)}, u32[]{:S(2)}) async-start(bf16[16,128,512]{2,1,0:T(8,128)(2,1)} %pad_maximum_fusion), calls=%async_computation | async-start | bytes 4194304 | tf_op jit(solution)/shard_map/all_to_all | solution.py:79
  24.1 3.7 %broadcast_compare_fusion.3 = (pred[512,2048]{0,1:T(8,128)(4,1)S(1)}, pred[512,2048]{0,1:T(8,128)(4,1)}, pred[512,2048]{0,1:T(8,128)(4,1)}, pred[512,2048]{0,1:T(8,128)(4,1)}) fusion(s32[512]{0:T(512)S(1)} %get-tuple-element.30, s32[2048]{0:T(1024)S(1)} %broadcast_bitcast_fusion, s32[512]{0:T(512)S(1)} %get-tuple-element.29, s32[512]{0:T(512)S(1)} %get-tuple-element.28, ...), kind=kLoop, calls=%fused_computation.45 | loop fusion | flops 4194304 | bytes 4210688 | tf_op jit(solution)/shard_map/eq | solution.py:30
  27.8 33.4 %all-to-all-done = bf16[16,128,512]{2,1,0:T(8,128)(2,1)S(1)} async-done(((bf16[16,128,512]{2,1,0:T(8,128)(2,1)}), bf16[16,128,512]{2,1,0:T(8,128)(2,1)S(1)}, u32[]{:S(2)}, u32[]{:S(2)}) %all-to-all-start) | async-done | bytes 2097184 | tf_op jit(solution)/shard_map/all_to_all | solution.py:79
  61.2 0.9 fusion.99
  62.1 1.7 slice.96
  63.8 1.7 slice.92
  65.6 1.7 slice.88
  67.3 0.8 slice.84
  68.1 1.0 fusion.100
  69.0 3.1 %fusion.11 = (f32[2,512]{1,0:T(2,128)S(1)}, f32[2048,512,2]{1,0,2:T(8,128)S(1)}) fusion(pred[512,2048]{0,1:T(8,128)(4,1)} %get-tuple-element.14, bf16[2048,128,1]{1,0,2:T(8,128)(2,1)S(1)} %bitcast.207, bf16[512,2,128]{2,1,0:T(2,128)(2,1)} %slice.96), kind=kOutput, calls=%fused_computation.20 | convolution fusion | flops 543161344 | bytes 10227712 | tf_op jit(solution)/shard_map/qgd,td->gqt/dot_general | solution.py:32
  72.2 2.2 fusion.10
  74.5 2.2 fusion.9
  76.7 2.2 fusion.8
  79.0 2.0 fusion.6
  81.0 2.0 fusion.4
  83.0 2.0 fusion.2
  85.0 2.2 fusion
  87.3 3.8 %fusion.51 = bf16[512,2,128]{0,2,1:T(8,128)(2,1)S(1)} fusion(bf16[2048,128,1]{1,0,2:T(8,128)(2,1)S(1)} %bitcast.203, f32[2048,512,2]{1,0,2:T(8,128)S(1)} %get-tuple-element.20, f32[2,512]{1,0:T(2,128)S(1)} %get-tuple-element.19, pred[512,2048]{0,1:T(8,128)(4,1)} %get-tuple-element.14, f32[512,2]{0,1:T(2,128)S(1)} %bitcast.222), kind=kOutput, calls=%fused_computation.58 | convolution fusion | flops 545521664 | bytes 10231808 | tf_op jit(solution)/shard_map/gqt,td->qgd/dot_general | solution.py:39
  91.1 3.8 %fusion.57 = bf16[512,2,128]{0,2,1:T(8,128)(2,1)S(1)} fusion(bf16[2048,128,1]{1,0,2:T(8,128)(2,1)S(1)} %bitcast.204, f32[2048,512,2]{1,0,2:T(8,128)S(1)} %get-tuple-element.22, f32[2,512]{1,0:T(2,128)S(1)} %get-tuple-element.21, pred[512,2048]{0,1:T(8,128)(4,1)} %get-tuple-element.13, f32[512,2]{0,1:T(2,128)S(1)} %bitcast.221), kind=kOutput, calls=%fused_computation.60 | convolution fusion | flops 545521664 | bytes 10231808 | tf_op jit(solution)/shard_map/gqt,td->qgd/dot_general | solution.py:39
  95.0 2.6 fusion.63
  97.6 2.6 fusion.69
  100.2 0.1 pad_maximum_fusion.1
  100.4 1.3 copy.49
  101.7 5.6 %all-to-all-start.1 = ((bf16[16,128,256]{2,1,0:T(8,128)(2,1)}), bf16[16,128,256]{2,1,0:T(8,128)(2,1)S(1)}, u32[]{:S(2)}, u32[]{:S(2)}) async-start(bf16[16,128,256]{2,1,0:T(8,128)(2,1)} %bitcast.44), calls=%async_computation.1 | async-start | bytes 2097152 | tf_op jit(solution)/shard_map/all_to_all | solution.py:87
  107.4 0.1 copy.51
  107.5 0.2 reduce-window.8
  107.6 0.1 add_reduce_fusion
  107.7 25.2 %all-to-all-done.1 = bf16[16,128,256]{2,1,0:T(8,128)(2,1)S(1)} async-done(((bf16[16,128,256]{2,1,0:T(8,128)(2,1)}), bf16[16,128,256]{2,1,0:T(8,128)(2,1)S(1)}, u32[]{:S(2)}, u32[]{:S(2)}) %all-to-all-start.1) | async-done | bytes 1048608 | tf_op jit(solution)/shard_map/all_to_all | solution.py:87
  133.0 0.2 convert_bitcast_fusion
  133.2 0.2 copy.62
  133.4 0.3 fusion.29
  133.7 1.1 convolution_convert_fusion
  134.9 16.3 %reshape.112 = bf16[16,3,28,4096]{3,2,1,0:T(8,128)(2,1)} reshape(bf16[5505024]{0:T(1024)(128)(2,1)} %all-gather.3.cloned.1.call-done) | data formatting | bytes 22020096 | tf_op jit(solution)/shard_map/reshape | solution.py:68
  151.2 27.0 %all-gather.5.cloned.1.call-done = bf16[640,4096]{1,0:T(8,128)(2,1)} async-done(((bf16[40,4096]{1,0:T(8,128)(2,1)}), bf16[640,4096]{1,0:T(8,128)(2,1)}) %all-gather.5.cloned.1.call-update) | async-done | bytes 5242896 | tf_op jit(solution)/shard_map/all_gather | solution.py:102
  178.3 10.7 %fusion.30 = f32[2,640,16,28]{1,3,0,2:T(8,128)S(1)} fusion(bf16[16,3,28,4096]{3,2,1,0:T(8,128)(2,1)} %reshape.112, bf16[640,4096]{1,0:T(8,128)(2,1)} %all-gather.5.cloned.1.call-done), kind=kOutput, calls=%fused_computation.46 | convolution fusion | flops 4697620480 | bytes 18546688 | tf_op jit(solution)/shard_map/rd,jkud->krju/dot_general | solution.py:103
  189.0 7.5 %bitcast_convert_fusion = bf16[640,4096]{1,0:T(8,128)(2,1)} fusion(bf16[16,3,28,4096]{3,2,1,0:T(8,128)(2,1)} %reshape.112, f32[2,640,16,28]{1,3,0,2:T(8,128)S(1)} %fusion.30), kind=kOutput, calls=%fused_computation | convolution fusion | flops 2353152000 | bytes 11730944 | tf_op jit(solution)/shard_map/rju,jud->rd/dot_general | solution.py:107
  196.6 63.8 %reduce-scatter.2.cloned.1.call-done = bf16[40,4096]{1,0:T(8,128)(2,1)} async-done(((bf16[640,4096]{1,0:T(8,128)(2,1)}), bf16[40,4096]{1,0:T(8,128)(2,1)}) %reduce-scatter.2.cloned.1.call-update) | async-done | bytes 327696 | tf_op jit(solution)/shard_map/reduce_scatter | solution.py:110
  260.4 2.4 fusion.16
  (42 shorter events, 0.7 us)
Async XLA Ops:
  6.5 7.4 %copy-start.3 = (bf16[1,128,4096]{2,1,0:T(8,128)(2,1)S(1)}, bf16[1,128,4096]{2,1,0:T(8,128)(2,1)}, u32[]{:S(2)}) copy-start(bf16[1,128,4096]{2,1,0:T(8,128)(2,1)} %param.9) | copy-start | bytes 3145732
  6.5 128.4 %all-gather.3.cloned.1.call-start = ((), (), s32[]{:S(2)}) async-start(), calls=%async_computation.3 | async-start | bytes 11698176 | tf_op jit(solution)/shard_map/all_gather | solution.py:67
  11.8 12.0 %copy-start.9 = (s32[1,16]{1,0:T(1,128)S(1)}, s32[1,16]{1,0:T(1,128)}, u32[]{:S(2)}) copy-start(s32[1,16]{1,0:T(1,128)} %param.12) | copy-start | bytes 196
  16.3 44.9 %all-to-all-start = ((bf16[16,128,512]{2,1,0:T(8,128)(2,1)}), bf16[16,128,512]{2,1,0:T(8,128)(2,1)S(1)}, u32[]{:S(2)}, u32[]{:S(2)}) async-start(bf16[16,128,512]{2,1,0:T(8,128)(2,1)} %pad_maximum_fusion), calls=%async_computation | async-start | bytes 4194304 | tf_op jit(solution)/shard_map/all_to_all | solution.py:79
  68.1 4.2 %copy-start.1 = (pred[512,2048]{0,1:T(8,128)(4,1)S(1)}, pred[512,2048]{0,1:T(8,128)(4,1)}, u32[]{:S(2)}) copy-start(pred[512,2048]{0,1:T(8,128)(4,1)} %get-tuple-element.13) | copy-start | bytes 3145732
  68.1 4.2 %copy-start.7 = (bf16[512,2,128]{2,1,0:T(2,128)(2,1)S(1)}, bf16[512,2,128]{2,1,0:T(2,128)(2,1)}, u32[]{:S(2)}) copy-start(bf16[512,2,128]{2,1,0:T(2,128)(2,1)} %slice.92) | copy-start | bytes 786436
  72.2 2.3 copy-start
  72.2 2.3 copy-start.6
  74.5 2.3 copy-start.5
  76.7 2.2 copy-start.2
  83.0 4.3 %copy-start.4 = (bf16[16,128,128]{2,1,0:T(8,128)(2,1)S(1)}, bf16[16,128,128]{2,1,0:T(8,128)(2,1)}, u32[]{:S(2)}) copy-start(bf16[16,128,128]{2,1,0:T(8,128)(2,1)} %get-tuple-element.10) | copy-start | bytes 1572868
  97.6 9.7 %copy-start.10 = (s32[1,128,2]{1,2,0:T(2,128)S(1)}, s32[1,128,2]{1,2,0:T(2,128)}, u32[]{:S(2)}) copy-start(s32[1,128,2]{1,2,0:T(2,128)} %param.13) | copy-start | bytes 3076
  100.2 33.5 %copy-start.8 = (f32[4096]{0:T(1024)S(1)}, f32[4096]{0:T(1024)}, u32[]{:S(2)}) copy-start(f32[4096]{0:T(1024)} %param.15) | copy-start | bytes 49156
  101.7 31.3 %all-to-all-start.1 = ((bf16[16,128,256]{2,1,0:T(8,128)(2,1)}), bf16[16,128,256]{2,1,0:T(8,128)(2,1)S(1)}, u32[]{:S(2)}, u32[]{:S(2)}) async-start(bf16[16,128,256]{2,1,0:T(8,128)(2,1)} %bitcast.44), calls=%async_computation.1 | async-start | bytes 2097152 | tf_op jit(solution)/shard_map/all_to_all | solution.py:87
  107.3 71.0 %all-gather.5.cloned.1.call-start = ((), (), s32[]{:S(2)}) async-start(), calls=%async_computation.4 | async-start | bytes 5570560 | tf_op jit(solution)/shard_map/all_gather | solution.py:102
  134.8 125.6 %reduce-scatter.2.cloned.1.call-start = ((), (), s32[]{:S(2)}) async-start(), calls=%async_computation.5 | async-start | bytes 5570560 | tf_op jit(solution)/shard_map/reduce_scatter | solution.py:110
  189.0 7.5 %copy-start.11 = (f32[1,128,2]{1,2,0:T(2,128)S(1)}, f32[1,128,2]{1,2,0:T(2,128)}, u32[]{:S(2)}) copy-start(f32[1,128,2]{1,2,0:T(2,128)} %param.14) | copy-start | bytes 3076
Sparse Core Ops, SparseCore 0:
  12.0 120.8 all-gather.2
  134.9 43.2 all-gather.4
  196.6 63.7 reduce-scatter.1

commit v8 on v7

--- a/solution.py
+++ b/solution.py
@@ -65,7 +65,9 @@
 
     weights_local = jnp.concatenate([w_in, w_down[None]], axis=0).reshape(-1)
     weights_flat = lax.all_gather(weights_local, "seq", axis=0, tiled=True)
-    weights_all = weights_flat.reshape((seq_count,) + (3,) + w_down.shape)
+    weights_all = jnp.transpose(
+        weights_flat.reshape((seq_count,) + (3,) + w_down.shape), (1, 0, 2, 3)
+    ).reshape(3, seq_count * w_down.shape[0], w_down.shape[1])
 
     query_send = jnp.transpose(query_rows[0].reshape(tok_count, seq_count, feat), (1, 0, 2))
     kv_repeat = seq_count // KVH
@@ -101,11 +103,11 @@
     ).astype(jnp.bfloat16)
     gathered = lax.all_gather(dispatched, "grp", axis=0, tiled=True)
     gate_up = jnp.einsum(
-        "rd,jkud->krju", gathered, weights_all[:, :2], preferred_element_type=jnp.float32
+        "rd,kud->kru", gathered, weights_all[:2], preferred_element_type=jnp.float32
     )
     hidden = (jax.nn.silu(gate_up[0]) * gate_up[1]).astype(jnp.bfloat16)
     terms = jnp.einsum(
-        "rju,jud->rd", hidden, weights_all[:, 2], preferred_element_type=jnp.float32
+        "ru,ud->rd", hidden, weights_all[2], preferred_element_type=jnp.float32
     )
     returned = lax.psum_scatter(
         terms.astype(jnp.bfloat16), "grp", scatter_dimension=0, tiled=True

time: 270 us -> 287 us (1.063); the launches traced: 269 us -> 282 us
  local copies, waits for them, and re-layouts: 32.2 us -> 64 us
  waiting for transfers between devices: 150 us -> 125 us
  matrix products: 44.5 us -> 49.6 us
    all_gather x1, waiting for transfers between devices: 27 us -> 0.01 us  [shards_body(): gathered = lax.all_gather(dispatched, 'grp', axis=0, tiled=True)]
    slice x0 -> x3, local copies, waits for them, and re-layouts: none -> 27 us  [the longest x2 22.3 us: shards_body(): weights_all[:2]]
    dot_general x2, matrix products: 18.2 us -> 23.3 us  [the longest x1 18.5 us: shards_body(): jnp.einsum('rd,kud->kru', gathered, weights_all[:2], preferred_element_ty...]
    squeeze x0 -> x1, local copies, waits for them, and re-layouts: none -> 4.82 us  [shards_body(): weights_all[2]]
  transfers between devices with their start and end apart: 5 -> 5, of which waited for: 4 -> 3; matrix products, arithmetic and copies ran while one was open for 25% -> 35% of each run, Pallas kernels for 0% -> 0%
where the time goes in v8:
time: 287 us; the launch traced here: 282 us
  waiting for transfers between devices  125 us (44%)
  local copies, waits for them, and re-layouts  64 us (22%)
  matrix products  49.6 us (17%)
  other arithmetic  16.4 us (6%)
  starting transfers between devices  13.7 us (5%)
  between operations  13.7 us (5%)
    reduce_scatter x1, waiting for transfers between devices, shards_body(): lax.psum_scatter(terms.astype(jnp.bfloat16), 'grp', scatter_dimension=0,...  66 us
    all_to_all x1, waiting for transfers between devices, shards_body(): packed_all = lax.all_to_all(packed, 'seq', 0, 0, tiled=False)  33.4 us
    all_to_all x1, waiting for transfers between devices, shards_body(): lax.all_to_all(attended.reshape(seq_count, tok_count, feat), 'seq', 0, 0,...  25.5 us
    slice x2, local copies, waits for them, and re-layouts, shards_body(): weights_all[:2]  22.3 us
    dot_general x1, matrix products, shards_body(): jnp.einsum('rd,kud->kru', gathered, weights_all[:2], preferred_element_ty...  18.5 us
    reshape x1, local copies, waits for them, and re-layouts, shards_body(): weights_flat.reshape((seq_count,) + (3,) + w_down.shape)  16.3 us
    dot_general x4, matrix products, attend(): jnp.einsum('gqt,td->qgd', weights.astype(jnp.bfloat16), value_all, prefer...  13 us
    dot_general x4, matrix products, attend(): jnp.einsum('qgd,td->gqt', query_tile, key_all, preferred_element_type=jnp...  9.79 us
  transfers between devices with their start and end apart: 5, of which 3 were waited for; matrix products, arithmetic and copies ran while one was open for 35% of the time, Pallas kernels for 0%

profile of v8, /device:TPU:2, one launch (start us, length us, event | category | flops | bytes accessed | tf_op | source)
XLA Modules:
  0.0 282.3 jit_solution(8750032997494611556)
XLA Ops:
  6.5 1.5 copy.54
  8.1 2.0 pad_maximum_fusion.2
  10.0 0.5 copy.55
  10.5 1.3 reshape.115
  11.8 1.0 copy.65
  12.9 1.0 copy.66
  13.9 0.2 copy.64
  14.2 0.3 copy.88
  14.7 1.6 pad_maximum_fusion
  16.3 8.0 %all-to-all-start = ((bf16[16,128,512]{2,1,0:T(8,128)(2,1)}), bf16[16,128,512]{2,1,0:T(8,128)(2,1)S(1)}, u32[]{:S(2)}, u32[]{:S(2)}) async-start(bf16[16,128,512]{2,1,0:T(8,128)(2,1)} %pad_maximum_fusion), calls=%async_computation | async-start | bytes 4194304 | tf_op jit(solution)/shard_map/all_to_all | solution.py:81
  24.7 3.7 %broadcast_compare_fusion.3 = (pred[512,2048]{0,1:T(8,128)(4,1)}, pred[512,2048]{0,1:T(8,128)(4,1)}, pred[512,2048]{0,1:T(8,128)(4,1)}, pred[512,2048]{0,1:T(8,128)(4,1)S(1)}) fusion(s32[512]{0:T(512)S(1)} %get-tuple-element.30, s32[2048]{0:T(1024)S(1)} %broadcast_bitcast_fusion, s32[512]{0:T(512)S(1)} %get-tuple-element.29, s32[512]{0:T(512)S(1)} %get-tuple-element.28, ...), kind=kLoop, calls=%fused_computation.45 | loop fusion | flops 4194304 | bytes 4210688 | tf_op jit(solution)/shard_map/eq | solution.py:30
  28.3 33.4 %all-to-all-done = bf16[16,128,512]{2,1,0:T(8,128)(2,1)S(1)} async-done(((bf16[16,128,512]{2,1,0:T(8,128)(2,1)}), bf16[16,128,512]{2,1,0:T(8,128)(2,1)S(1)}, u32[]{:S(2)}, u32[]{:S(2)}) %all-to-all-start) | async-done | bytes 2097184 | tf_op jit(solution)/shard_map/all_to_all | solution.py:81
  61.7 0.9 fusion.102
  62.6 1.7 slice.88
  64.3 1.7 slice.100
  66.0 1.7 slice.96
  67.8 0.8 slice.92
  68.6 1.0 fusion.103
  69.5 3.1 %fusion.10 = (f32[2,512]{1,0:T(2,128)S(1)}, f32[2048,512,2]{1,0,2:T(8,128)S(1)}) fusion(pred[512,2048]{0,1:T(8,128)(4,1)} %get-tuple-element.11, bf16[2048,128,1]{1,0,2:T(8,128)(2,1)S(1)} %bitcast.205, bf16[512,2,128]{2,1,0:T(2,128)(2,1)} %slice.88), kind=kOutput, calls=%fused_computation.18 | convolution fusion | flops 543161344 | bytes 10227712 | tf_op jit(solution)/shard_map/qgd,td->gqt/dot_general | solution.py:32
  72.7 2.2 fusion.11
  75.0 2.2 fusion.12
  77.2 2.2 fusion.13
  79.4 2.0 fusion
  81.5 2.0 fusion.2
  83.5 2.0 fusion.4
  85.5 2.2 fusion.6
  87.7 3.9 %fusion.72 = bf16[512,2,128]{0,2,1:T(8,128)(2,1)S(1)} fusion(bf16[2048,128,1]{1,0,2:T(8,128)(2,1)S(1)} %bitcast.201, f32[2048,512,2]{1,0,2:T(8,128)S(1)} %get-tuple-element.26, f32[2,512]{1,0:T(2,128)S(1)} %get-tuple-element.25, pred[512,2048]{0,1:T(8,128)(4,1)} %get-tuple-element.11, f32[512,2]{0,1:T(2,128)S(1)} %bitcast.220), kind=kOutput, calls=%fused_computation.64 | convolution fusion | flops 545521664 | bytes 10231808 | tf_op jit(solution)/shard_map/gqt,td->qgd/dot_general | solution.py:39
  91.6 3.9 %fusion.66 = bf16[512,2,128]{0,2,1:T(8,128)(2,1)S(1)} fusion(bf16[2048,128,1]{1,0,2:T(8,128)(2,1)S(1)} %bitcast.202, f32[2048,512,2]{1,0,2:T(8,128)S(1)} %get-tuple-element.24, f32[2,512]{1,0:T(2,128)S(1)} %get-tuple-element.23, pred[512,2048]{0,1:T(8,128)(4,1)} %get-tuple-element.12, f32[512,2]{0,1:T(2,128)S(1)} %bitcast.219), kind=kOutput, calls=%fused_computation.62 | convolution fusion | flops 545521664 | bytes 10231808 | tf_op jit(solution)/shard_map/gqt,td->qgd/dot_general | solution.py:39
  95.5 2.6 fusion.60
  98.1 2.6 fusion.54
  100.8 1.3 copy.51
  102.2 5.6 %all-to-all-start.1 = ((bf16[16,128,256]{2,1,0:T(8,128)(2,1)}), bf16[16,128,256]{2,1,0:T(8,128)(2,1)S(1)}, u32[]{:S(2)}, u32[]{:S(2)}) async-start(bf16[16,128,256]{2,1,0:T(8,128)(2,1)} %bitcast.44), calls=%async_computation.1 | async-start | bytes 2097152 | tf_op jit(solution)/shard_map/all_to_all | solution.py:89
  107.8 0.1 copy.53
  107.9 0.2 reduce-window.8
  108.2 25.5 %all-to-all-done.1 = bf16[16,128,256]{2,1,0:T(8,128)(2,1)S(1)} async-done(((bf16[16,128,256]{2,1,0:T(8,128)(2,1)}), bf16[16,128,256]{2,1,0:T(8,128)(2,1)S(1)}, u32[]{:S(2)}, u32[]{:S(2)}) %all-to-all-start.1) | async-done | bytes 1048608 | tf_op jit(solution)/shard_map/all_to_all | solution.py:89
  133.7 0.2 convert_bitcast_fusion
  133.9 0.2 copy.63
  134.1 0.3 fusion.30
  134.4 1.1 convolution_convert_fusion.1
  135.7 16.3 %reshape.116 = bf16[16,3,28,4096]{3,2,1,0:T(8,128)(2,1)} reshape(bf16[5505024]{0:T(1024)(128)(2,1)} %all-gather.3.cloned.1.call-done) | data formatting | bytes 22020096 | tf_op jit(solution)/shard_map/reshape | solution.py:69
  151.9 4.7 %slice.115 = bf16[1,16,28,4096]{3,2,0,1:T(8,128)(2,1)} slice(bf16[3,16,28,4096]{3,2,0,1:T(8,128)(2,1)} %bitcast.189), slice={[2:3], [0:16], [0:28], [0:4096]} | slice | bytes 7340032 | tf_op jit(solution)/shard_map/slice | solution.py:110
  156.6 7.8 %slice.112 = bf16[2,16,28,4096]{3,2,0,1:T(8,128)(2,1)} slice(bf16[3,16,28,4096]{3,2,0,1:T(8,128)(2,1)} %bitcast.190), slice={[0:2], [0:16], [0:28], [0:4096]} | slice | bytes 14680064 | tf_op jit(solution)/shard_map/slice | solution.py:106
  164.4 14.5 %copy.56 = bf16[2,16,28,4096]{3,0,2,1:T(2,128)(2,1)} copy(bf16[2,16,28,4096]{3,2,0,1:T(8,128)(2,1)} %slice.112) | data formatting | bytes 14680064 | tf_op jit(solution)/shard_map/slice | solution.py:106
  178.9 4.8 %squeeze.5 = bf16[448,4096]{1,0:T(8,128)(2,1)} reshape(bf16[1,16,28,4096]{3,2,0,1:T(8,128)(2,1)} %slice.115) | data formatting | bytes 7340032 | tf_op jit(solution)/shard_map/squeeze | solution.py:110
  183.8 18.5 %fusion.31 = f32[2,640,448]{1,2,0:T(8,128)S(1)} fusion(bf16[640,4096]{1,0:T(8,128)(2,1)} %all-gather.5.cloned.1.call-done, bf16[2,448,4096]{2,0,1:T(2,128)(2,1)} %bitcast.193), kind=kOutput, calls=%fused_computation.46 | convolution fusion | flops 4697620480 | bytes 14876672 | tf_op jit(solution)/shard_map/rd,kud->kru/dot_general | solution.py:105
  202.3 4.7 %convolution_convert_fusion = bf16[640,4096]{1,0:T(8,128)(2,1)} fusion(bf16[448,4096]{1,0:T(8,128)(2,1)S(1)} %copy-done.3, f32[2,640,448]{1,2,0:T(8,128)S(1)} %fusion.31), kind=kOutput, calls=%fused_computation.22 | convolution fusion | flops 2353152000 | bytes 11206656 | tf_op jit(solution)/shard_map/ru,ud->rd/dot_general | solution.py:109
  207.1 66.0 %reduce-scatter.2.cloned.1.call-done = bf16[40,4096]{1,0:T(8,128)(2,1)} async-done(((bf16[640,4096]{1,0:T(8,128)(2,1)}), bf16[40,4096]{1,0:T(8,128)(2,1)}) %reduce-scatter.2.cloned.1.call-update) | async-done | bytes 327696 | tf_op jit(solution)/shard_map/reduce_scatter | solution.py:112
  273.1 2.4 fusion.17
  (48 shorter events, 1.0 us)
Async XLA Ops:
  6.5 7.4 %copy-start.4 = (bf16[1,128,4096]{2,1,0:T(8,128)(2,1)S(1)}, bf16[1,128,4096]{2,1,0:T(8,128)(2,1)}, u32[]{:S(2)}) copy-start(bf16[1,128,4096]{2,1,0:T(8,128)(2,1)} %param.9) | copy-start | bytes 3145732
  6.5 129.1 %all-gather.3.cloned.1.call-start = ((), (), s32[]{:S(2)}) async-start(), calls=%async_computation.3 | async-start | bytes 11698176 | tf_op jit(solution)/shard_map/all_gather | solution.py:67
  11.8 12.6 %copy-start.10 = (s32[1,16]{1,0:T(1,128)S(1)}, s32[1,16]{1,0:T(1,128)}, u32[]{:S(2)}) copy-start(s32[1,16]{1,0:T(1,128)} %param.12) | copy-start | bytes 196
  16.3 45.4 %all-to-all-start = ((bf16[16,128,512]{2,1,0:T(8,128)(2,1)}), bf16[16,128,512]{2,1,0:T(8,128)(2,1)S(1)}, u32[]{:S(2)}, u32[]{:S(2)}) async-start(bf16[16,128,512]{2,1,0:T(8,128)(2,1)} %pad_maximum_fusion), calls=%async_computation | async-start | bytes 4194304 | tf_op jit(solution)/shard_map/all_to_all | solution.py:81
  68.5 4.1 %copy-start.1 = (pred[512,2048]{0,1:T(8,128)(4,1)S(1)}, pred[512,2048]{0,1:T(8,128)(4,1)}, u32[]{:S(2)}) copy-start(pred[512,2048]{0,1:T(8,128)(4,1)} %get-tuple-element.12) | copy-start | bytes 3145732
  68.6 4.2 %copy-start.8 = (bf16[512,2,128]{2,1,0:T(2,128)(2,1)S(1)}, bf16[512,2,128]{2,1,0:T(2,128)(2,1)}, u32[]{:S(2)}) copy-start(bf16[512,2,128]{2,1,0:T(2,128)(2,1)} %slice.92) | copy-start | bytes 786436
  72.7 2.3 copy-start
  72.7 2.3 copy-start.7
  74.9 2.3 copy-start.6
  77.2 2.2 copy-start.2
  83.5 4.2 %copy-start.5 = (bf16[16,128,128]{2,1,0:T(8,128)(2,1)S(1)}, bf16[16,128,128]{2,1,0:T(8,128)(2,1)}, u32[]{:S(2)}) copy-start(bf16[16,128,128]{2,1,0:T(8,128)(2,1)} %get-tuple-element.10) | copy-start | bytes 1572868
  98.1 9.7 %copy-start.11 = (s32[1,128,2]{1,2,0:T(2,128)S(1)}, s32[1,128,2]{1,2,0:T(2,128)}, u32[]{:S(2)}) copy-start(s32[1,128,2]{1,2,0:T(2,128)} %param.13) | copy-start | bytes 3076
  100.7 33.7 %copy-start.9 = (f32[4096]{0:T(1024)S(1)}, f32[4096]{0:T(1024)}, u32[]{:S(2)}) copy-start(f32[4096]{0:T(1024)} %param.15) | copy-start | bytes 49156
  102.2 31.6 %all-to-all-start.1 = ((bf16[16,128,256]{2,1,0:T(8,128)(2,1)}), bf16[16,128,256]{2,1,0:T(8,128)(2,1)S(1)}, u32[]{:S(2)}, u32[]{:S(2)}) async-start(bf16[16,128,256]{2,1,0:T(8,128)(2,1)} %bitcast.44), calls=%async_computation.1 | async-start | bytes 2097152 | tf_op jit(solution)/shard_map/all_to_all | solution.py:89
  107.7 76.0 %all-gather.5.cloned.1.call-start = ((), (), s32[]{:S(2)}) async-start(), calls=%async_computation.4 | async-start | bytes 5570560 | tf_op jit(solution)/shard_map/all_gather | solution.py:104
  135.6 137.5 %reduce-scatter.2.cloned.1.call-start = ((), (), s32[]{:S(2)}) async-start(), calls=%async_computation.5 | async-start | bytes 5570560 | tf_op jit(solution)/shard_map/reduce_scatter | solution.py:112
  183.8 18.5 %copy-start.3 = (bf16[448,4096]{1,0:T(8,128)(2,1)S(1)}, bf16[448,4096]{1,0:T(8,128)(2,1)}, u32[]{:S(2)}) copy-start(bf16[448,4096]{1,0:T(8,128)(2,1)} %squeeze.5) | copy-start | bytes 11010052
  202.3 4.8 %copy-start.12 = (f32[1,128,2]{1,2,0:T(2,128)S(1)}, f32[1,128,2]{1,2,0:T(2,128)}, u32[]{:S(2)}) copy-start(f32[1,128,2]{1,2,0:T(2,128)} %param.14) | copy-start | bytes 3076
Sparse Core Ops, SparseCore 0:
  12.0 122.1 all-gather.2
  135.9 43.2 all-gather.4
  207.2 65.8 reduce-scatter.1
